TPU v7x, 32 devices: a whole 2x2x4 slice. The times are simulated.
32 devices in a mesh: group: 2 (over y), seq: 4 (over z), batch: 2 (over x), chan: 2 (over core).
Axes of the slice: x: 2, y: 2, z: 4, core: 2. Of those that a mesh axis runs over, the one named last changes fastest.
Arguments:
- history: bfloat16 [8, 1024, 4096], P(('group', 'batch'), 'seq', 'chan'), parts along dimension 0, may hold values from -6 to 6
- filter_taps: bfloat16 [1024, 4096], P('seq', 'chan'), may hold values from -0.1875 to 0.1875
- lengths: int32 [8], P(('group', 'batch')), parts along dimension 0, may hold values from 256 to 1024, as said below
- inner_gate: bfloat16 [8, 256, 4096], P(('group', 'batch'), 'seq', 'chan'), parts along dimension 0, may hold values from -6 to 6
- values_in: bfloat16 [8, 256, 4096], P(('group', 'batch'), 'seq', 'chan'), parts along dimension 0, may hold values from -6 to 6
- outer_gate: bfloat16 [8, 256, 4096], P(('group', 'batch'), 'seq', 'chan'), parts along dimension 0, may hold values from -6 to 6
- skip_gain: float32 [4096], P('chan'), may hold values from -4 to 4
Outputs:
- mixed: bfloat16 [8, 256, 4096], P(('group', 'batch'), 'seq', 'chan'), parts along dimension 0
- next_history: bfloat16 [8, 1024, 4096], P(('group', 'batch'), 'seq', 'chan'), parts along dimension 0
There are 2 independent parts, one for each index of `group`. A program takes and returns all parts, laid end to end along the dimension named above; an argument that names none is the same for every part. Nothing has to cross between parts.
Inputs may be any that keep to these rules, and one draw needn't show every extreme that they name: `lengths`: each request's prefilled length is a multiple of 256; some request of every part has exactly 1024, and some other is shorter.
All inputs are finite; a program needn't handle non-finite values.
Results may differ from a plain program's by a relative error of at most 0.0044.
Values may be sent and summed in bfloat16 or wider, within the bound.
No kernel may reach another device: no remote copies, remote signals or barrier semaphores. Data moves between devices by JAX's collectives and lax.ppermute only.
A program may use at most 128 MiB of HBM per device.

v0:
```python
import jax
import jax.numpy as jnp
from jax import lax
from jax.sharding import PartitionSpec as P

CHANNEL_CHUNKS = 4


def from_behind(block, axis, distance):
    devices = range(lax.axis_size(axis))
    route = [(i - distance, i) for i in devices if i - distance in devices]
    return lax.ppermute(block, axis, route)


def correlate(signal, kernel):
    width = signal.shape[2]
    return lax.conv_general_dilated(
        signal,
        kernel[:, None, :],
        (1,),
        "VALID",
        dimension_numbers=("NWC", "WIO", "NWC"),
        feature_group_count=width,
        preferred_element_type=jnp.float32,
    )


def per_device(history, filter_taps, lengths, inner_gate, values_in, outer_gate, skip_gain):
    position = lax.axis_index("seq")
    n_seq = lax.axis_size("seq")
    requests, tile_len, width = history.shape
    own_tokens = inner_gate.shape[1]
    span_len = own_tokens * n_seq
    assert span_len == tile_len
    chunk = width // CHANNEL_CHUNKS
    product_own = (inner_gate.astype(jnp.float32) * values_in.astype(jnp.float32)).astype(
        jnp.bfloat16
    )
    token_ids = jnp.arange(own_tokens, dtype=jnp.int32)
    exchange = (token_ids[:, None] + token_ids[None, :] == own_tokens - 1).astype(jnp.bfloat16)
    product_own = lax.optimization_barrier(product_own)
    product_rev = jnp.einsum(
        "ik,rkc->ric", exchange, product_own, preferred_element_type=jnp.float32
    ).astype(jnp.bfloat16)
    from_each = [product_rev] + [
        lax.ppermute(product_rev, "seq", [(d, 0)]) for d in range(1, n_seq)
    ]
    row_ids = position * tile_len + jnp.arange(tile_len, dtype=jnp.int32)
    live_rows = jnp.where(
        (row_ids[None, :] < lengths[:, None])[:, :, None], history, jnp.zeros_like(history)
    )
    prev_keep = ((row_ids - tile_len)[None, :] < lengths[:, None])[:, :, None]

    head_parts = []
    own_parts = []
    for c in range(CHANNEL_CHUNKS):
        cols = slice(c * chunk, (c + 1) * chunk)
        sent = from_behind(history[:, :, cols], "seq", 1)
        if own_parts:
            sent, _ = lax.optimization_barrier((sent, last_partial))
        head_first = jnp.concatenate([part[:, :, cols] for part in from_each[::-1]], axis=1)
        head_c = jnp.where(position == 0, head_first, sent)
        head_parts.append(head_c)
        prev_live = jnp.where(prev_keep, head_c, jnp.zeros_like(head_c))
        segment = jnp.concatenate([prev_live, live_rows[:, : tile_len - 1, cols]], axis=1)
        partial_rev = correlate(segment, filter_taps[:, cols])
        last_partial = partial_rev
        blocks = partial_rev.reshape(requests, n_seq, own_tokens, chunk)[:, ::-1]
        if own_parts:
            blocks, _ = lax.optimization_barrier((blocks, own_parts[-1]))
        reduced = lax.psum_scatter(blocks, "seq", scatter_dimension=1, tiled=True)
        own_parts.append(reduced[:, 0])
    summed = jnp.concatenate(own_parts, axis=2)[:, ::-1]
    product_float = product_own.astype(jnp.float32)
    total = summed + skip_gain[None, None, :] * product_float
    mixed = (outer_gate.astype(jnp.float32) * total).astype(jnp.bfloat16)
    next_history = jnp.concatenate(head_parts, axis=2)
    return (mixed, next_history)


def solution(mesh):
    in_specs = (
        P(("group", "batch"), "seq", "chan"),
        P("seq", "chan"),
        P(("group", "batch")),
        P(("group", "batch"), "seq", "chan"),
        P(("group", "batch"), "seq", "chan"),
        P(("group", "batch"), "seq", "chan"),
        P("chan"),
    )
    out_specs = (P(("group", "batch"), "seq", "chan"), P(("group", "batch"), "seq", "chan"))
    return jax.shard_map(
        per_device, mesh=mesh, in_specs=in_specs, out_specs=out_specs, check_vma=False
    )
```

profile of v0, /device:TPU:0, one launch (start us, length us, event | category | flops | bytes accessed | tf_op | source)
XLA Modules:
  0.0 221.6 jit_solution(17672727465125620940)
XLA Ops:
  7.2 1.5 multiply_convert_fusion.1
  9.8 1.3 collective-permute-start.2
  11.1 1.3 collective-permute-start.1
  12.4 1.3 collective-permute-start
  13.7 1.4 fusion.17
  15.0 6.8 %collective-permute-start.3 = (bf16[2,256,512]{2,1,0:T(8,128)(2,1)}, bf16[2,256,512]{2,1,0:T(8,128)(2,1)}, u32[]{:S(2)}, u32[]{:S(2)}) collective-permute-start(bf16[2,256,512]{2,1,0:T(8,128)(2,1)} %get-tuple-element.22), channel_id=1, source_target_pairs={{0,4},{4,8},{8,12},{1,5},{5,9},{9,13},{2,6},{6,10},{10,14},{3,7},{... | collective-permute-start | bytes 1572872 | tf_op jit(solution)/shard_map/ppermute | solution.py:12
  21.9 3.5 %collective-permute-start.4 = (bf16[2,256,512]{2,1,0:T(8,128)(2,1)}, bf16[2,256,512]{2,1,0:T(8,128)(2,1)}, u32[]{:S(2)}, u32[]{:S(2)}) collective-permute-start(bf16[2,256,512]{2,1,0:T(8,128)(2,1)} %get-tuple-element.23), channel_id=1, source_target_pairs={{0,4},{4,8},{8,12},{1,5},{5,9},{9,13},{2,6},{6,10},{10,14},{3,7},{... | collective-permute-start | bytes 1572872 | tf_op jit(solution)/shard_map/ppermute | solution.py:12
  28.6 20.0 %collective-permute-done.2 = bf16[2,64,2048]{2,1,0:T(8,128)(2,1)} collective-permute-done((bf16[2,64,2048]{2,1,0:T(8,128)(2,1)S(1)}, bf16[2,64,2048]{2,1,0:T(8,128)(2,1)}, u32[]{:S(2)}, u32[]{:S(2)}) %collective-permute-start.2) | collective-permute-done | bytes 524320 | tf_op jit(solution)/shard_map/ppermute | solution.py:46
  48.6 2.1 collective-permute-start.6
  50.7 1.8 fusion.21
  52.6 2.1 collective-permute-start.5
  54.6 1.8 fusion.20
  56.5 1.9 fusion.19
  59.4 29.1 %fusion.7 = f32[2,256,512]{2,0,1:T(2,128)S(1)} fusion(bf16[2,511,512]{2,1,0:T(8,128)(2,1)S(1)} %pad_maximum_fusion.1, bf16[256,1,512]{2,0,1:T(8,128)(2,1)S(1)} %get-tuple-element.32), kind=kOutput, calls=%fused_computation.17 | convolution fusion | flops 134217728 | bytes 2357248 | tf_op jit(solution)/shard_map/conv_general_dilated | solution.py:17
  90.1 1.3 broadcast_select_fusion.3
  91.6 29.1 %fusion.5 = f32[2,256,512]{2,0,1:T(2,128)S(1)} fusion(bf16[2,511,512]{2,1,0:T(8,128)(2,1)S(1)} %pad_maximum_fusion.2, bf16[256,1,512]{2,0,1:T(8,128)(2,1)S(1)} %copy-done.12), kind=kOutput, calls=%fused_computation.15 | convolution fusion | flops 134217728 | bytes 2357248 | tf_op jit(solution)/shard_map/conv_general_dilated | solution.py:17
  121.0 1.1 rev.16
  122.7 28.9 %fusion.3 = f32[2,256,512]{2,0,1:T(2,128)S(1)} fusion(bf16[2,511,512]{2,1,0:T(8,128)(2,1)S(1)} %pad_maximum_fusion.3, bf16[256,1,512]{2,0,1:T(8,128)(2,1)} %get-tuple-element.33), kind=kOutput, calls=%fused_computation.13 | convolution fusion | flops 134217728 | bytes 2357248 | tf_op jit(solution)/shard_map/conv_general_dilated | solution.py:17
  152.8 1.1 broadcast_select_fusion.1
  154.9 29.1 %fusion.1 = f32[2,256,512]{2,0,1:T(2,128)S(1)} fusion(bf16[2,511,512]{2,1,0:T(8,128)(2,1)S(1)} %pad_maximum_fusion.4, bf16[256,1,512]{2,0,1:T(8,128)(2,1)S(1)} %copy-done.10), kind=kOutput, calls=%fused_computation.11 | convolution fusion | flops 134217728 | bytes 2357248 | tf_op jit(solution)/shard_map/conv_general_dilated | solution.py:17
  184.2 1.1 rev.18
  185.3 1.6 pad_maximum_fusion
  187.0 25.4 %reduce-scatter.11.cloned.1.call-done = f32[2,1,64,512]{3,2,0,1:T(8,128)} async-done(((f32[2,4,64,512]{3,2,0,1:T(8,128)}), f32[2,1,64,512]{3,2,0,1:T(8,128)}) %reduce-scatter.11.cloned.1.call-update) | async-done | bytes 262160 | tf_op jit(solution)/shard_map/reduce_scatter | solution.py:71
  212.4 1.1 pad_maximum_fusion.5
  (72 shorter events, 11.6 us)
Async XLA Ops:
  7.2 6.5 %copy-start = (bf16[2,256,2048]{2,1,0:T(8,128)(2,1)S(1)}, bf16[2,256,2048]{2,1,0:T(8,128)(2,1)}, u32[]{:S(2)}) copy-start(bf16[2,256,2048]{2,1,0:T(8,128)(2,1)} %param.7) | copy-start | bytes 6291460
  7.2 115.2 %reduce-scatter.5.cloned.1.call-start = ((), (), s32[]{:S(2)}) async-start(), calls=%async_computation.4 | async-start | bytes 1310720 | tf_op jit(solution)/shard_map/reduce_scatter | solution.py:71
  9.8 15.6 %copy-start.16 = (s32[2]{0:T(128)S(1)}, s32[2]{0:T(128)}, u32[]{:S(2)}) copy-start(s32[2]{0:T(128)} %param.9) | copy-start | bytes 28
  9.8 38.8 %collective-permute-start.2 = (bf16[2,64,2048]{2,1,0:T(8,128)(2,1)S(1)}, bf16[2,64,2048]{2,1,0:T(8,128)(2,1)}, u32[]{:S(2)}, u32[]{:S(2)}) collective-permute-start(bf16[2,64,2048]{2,1,0:T(8,128)(2,1)S(1)} %fusion), channel_id=1, source_target_pairs={{4,0},{5,1},{6,2},{7,3},{20,16},{21,17},{22,18},{23,19}} | collective-permute-start | bytes 1572872 | tf_op jit(solution)/shard_map/ppermute | solution.py:46
  11.1 41.5 %collective-permute-start.1 = (bf16[2,64,2048]{2,1,0:T(8,128)(2,1)S(1)}, bf16[2,64,2048]{2,1,0:T(8,128)(2,1)}, u32[]{:S(2)}, u32[]{:S(2)}) collective-permute-start(bf16[2,64,2048]{2,1,0:T(8,128)(2,1)S(1)} %fusion), channel_id=1, source_target_pairs={{8,0},{9,1},{10,2},{11,3},{24,16},{25,17},{26,18},{27,19}} | collective-permute-start | bytes 1572872 | tf_op jit(solution)/shard_map/ppermute | solution.py:46
  12.4 44.1 %collective-permute-start = (bf16[2,64,2048]{2,1,0:T(8,128)(2,1)S(1)}, bf16[2,64,2048]{2,1,0:T(8,128)(2,1)}, u32[]{:S(2)}, u32[]{:S(2)}) collective-permute-start(bf16[2,64,2048]{2,1,0:T(8,128)(2,1)S(1)} %fusion), channel_id=1, source_target_pairs={{12,0},{13,1},{14,2},{15,3},{28,16},{29,17},{30,18},{31,19}} | collective-permute-start | bytes 1572872 | tf_op jit(solution)/shard_map/ppermute | solution.py:46
  15.0 43.3 %collective-permute-start.3 = (bf16[2,256,512]{2,1,0:T(8,128)(2,1)}, bf16[2,256,512]{2,1,0:T(8,128)(2,1)}, u32[]{:S(2)}, u32[]{:S(2)}) collective-permute-start(bf16[2,256,512]{2,1,0:T(8,128)(2,1)} %get-tuple-element.22), channel_id=1, source_target_pairs={{0,4},{4,8},{8,12},{1,5},{5,9},{9,13},{2,6},{6,10},{10,14},{3,7},{... | collective-permute-start | bytes 1572872 | tf_op jit(solution)/shard_map/ppermute | solution.py:12
  21.9 66.7 %collective-permute-start.4 = (bf16[2,256,512]{2,1,0:T(8,128)(2,1)}, bf16[2,256,512]{2,1,0:T(8,128)(2,1)}, u32[]{:S(2)}, u32[]{:S(2)}) collective-permute-start(bf16[2,256,512]{2,1,0:T(8,128)(2,1)} %get-tuple-element.23), channel_id=1, source_target_pairs={{0,4},{4,8},{8,12},{1,5},{5,9},{9,13},{2,6},{6,10},{10,14},{3,7},{... | collective-permute-start | bytes 1572872 | tf_op jit(solution)/shard_map/ppermute | solution.py:12
  48.6 102.9 %collective-permute-start.6 = (bf16[2,256,512]{2,1,0:T(8,128)(2,1)}, bf16[2,256,512]{2,1,0:T(8,128)(2,1)}, u32[]{:S(2)}, u32[]{:S(2)}) collective-permute-start(bf16[2,256,512]{2,1,0:T(8,128)(2,1)} %get-tuple-element.24), channel_id=1, source_target_pairs={{0,4},{4,8},{8,12},{1,5},{5,9},{9,13},{2,6},{6,10},{10,14},{3,7},{... | collective-permute-start | bytes 1572872 | tf_op jit(solution)/shard_map/ppermute | solution.py:12
  52.6 68.1 %collective-permute-start.5 = (bf16[2,256,512]{2,1,0:T(8,128)(2,1)}, bf16[2,256,512]{2,1,0:T(8,128)(2,1)}, u32[]{:S(2)}, u32[]{:S(2)}) collective-permute-start(bf16[2,256,512]{2,1,0:T(8,128)(2,1)} %get-tuple-element.25), channel_id=1, source_target_pairs={{0,4},{4,8},{8,12},{1,5},{5,9},{9,13},{2,6},{6,10},{10,14},{3,7},{... | collective-permute-start | bytes 1572872 | tf_op jit(solution)/shard_map/ppermute | solution.py:12
  89.9 64.1 %reduce-scatter.7.cloned.1.call-start = ((), (), s32[]{:S(2)}) async-start(), calls=%async_computation.5 | async-start | bytes 1310720 | tf_op jit(solution)/shard_map/reduce_scatter | solution.py:71
  90.1 1.4 copy-start.12
  120.7 1.3 copy-start.6
  120.7 1.3 copy-start.7
  120.7 1.3 copy-start.8
  120.7 1.3 copy-start.9
  122.4 62.9 %reduce-scatter.9.cloned.1.call-start = ((), (), s32[]{:S(2)}) async-start(), calls=%async_computation.6 | async-start | bytes 1310720 | tf_op jit(solution)/shard_map/reduce_scatter | solution.py:71
  154.0 58.3 %reduce-scatter.11.cloned.1.call-start = ((), (), s32[]{:S(2)}) async-start(), calls=%async_computation.7 | async-start | bytes 1310720 | tf_op jit(solution)/shard_map/reduce_scatter | solution.py:71
  185.3 27.1 %copy-start.11 = (f32[2,1,64,512]{3,2,0,1:T(8,128)S(1)}, f32[2,1,64,512]{3,2,0,1:T(8,128)}, u32[]{:S(2)}) copy-start(f32[2,1,64,512]{3,2,0,1:T(8,128)} %reduce-scatter.5.cloned.1.call-done) | copy-start | bytes 786436
  185.3 27.1 %copy-start.13 = (f32[2,1,64,512]{3,2,0,1:T(8,128)S(1)}, f32[2,1,64,512]{3,2,0,1:T(8,128)}, u32[]{:S(2)}) copy-start(f32[2,1,64,512]{3,2,0,1:T(8,128)} %reduce-scatter.7.cloned.1.call-done) | copy-start | bytes 786436
  185.3 27.1 %copy-start.14 = (f32[2,1,64,512]{3,2,0,1:T(8,128)S(1)}, f32[2,1,64,512]{3,2,0,1:T(8,128)}, u32[]{:S(2)}) copy-start(f32[2,1,64,512]{3,2,0,1:T(8,128)} %reduce-scatter.9.cloned.1.call-done) | copy-start | bytes 786436
  212.4 1.6 copy-start.2
  212.4 1.6 copy-start.5
  212.4 1.6 copy-start.15
  (4 other events, 4.1 us)
Sparse Core Ops, SparseCore 0:
  90.0 26.1 reduce-scatter.4
  122.5 26.7 reduce-scatter.6
  154.2 26.9 reduce-scatter.8
  185.4 26.9 reduce-scatter.10
where the time goes:
time: 222 us
  matrix products  117 us (53%)
  waiting for transfers between devices  45.6 us (21%)
  starting transfers between devices  19.3 us (9%)
  local copies, waits for them, and re-layouts  16.7 us (8%)
  between operations  14.2 us (6%)
  other arithmetic  9.39 us (4%)
    conv_general_dilated x4, matrix products, correlate(): lax.conv_general_dilated(signal, kernel[:, None, :], (1,), 'VALID', dimen...  116 us
    reduce_scatter x4, waiting for transfers between devices, per_device(): reduced = lax.psum_scatter(blocks, 'seq', scatter_dimension=1, tiled=True)  25.5 us
    ppermute x3, waiting for transfers between devices, per_device(): lax.ppermute(product_rev, 'seq', [(d, 0)])  20 us
    ppermute x4, starting transfers between devices, from_behind(): return lax.ppermute(block, axis, route)  14.6 us
    slice x4, local copies, waits for them, and re-layouts, per_device(): part[:, :, cols]  6.28 us
  transfers between devices with their start and end apart: 11, of which 2 were waited for; matrix products, arithmetic and copies ran while one was open for 61% of the time, Pallas kernels for 0%

commit v1 on v0

--- a/solution.py
+++ b/solution.py
@@ -42,8 +42,11 @@
     product_rev = jnp.einsum(
         "ik,rkc->ric", exchange, product_own, preferred_element_type=jnp.float32
     ).astype(jnp.bfloat16)
-    from_each = [product_rev] + [
-        lax.ppermute(product_rev, "seq", [(d, 0)]) for d in range(1, n_seq)
+    first_each = [product_rev[:, :, :chunk]] + [
+        lax.ppermute(product_rev[:, :, :chunk], "seq", [(d, 0)]) for d in range(1, n_seq)
+    ]
+    rest_each = [product_rev[:, :, chunk:]] + [
+        lax.ppermute(product_rev[:, :, chunk:], "seq", [(d, 0)]) for d in range(1, n_seq)
     ]
     row_ids = position * tile_len + jnp.arange(tile_len, dtype=jnp.int32)
     live_rows = jnp.where(
@@ -57,8 +60,13 @@
         cols = slice(c * chunk, (c + 1) * chunk)
         sent = from_behind(history[:, :, cols], "seq", 1)
         if own_parts:
-            sent, _ = lax.optimization_barrier((sent, last_partial))
-        head_first = jnp.concatenate([part[:, :, cols] for part in from_each[::-1]], axis=1)
+            (sent, rest_each), _ = lax.optimization_barrier(((sent, rest_each), last_partial))
+            rest_cols = slice((c - 1) * chunk, c * chunk)
+            head_first = jnp.concatenate(
+                [part[:, :, rest_cols] for part in rest_each[::-1]], axis=1
+            )
+        else:
+            head_first = jnp.concatenate(first_each[::-1], axis=1)
         head_c = jnp.where(position == 0, head_first, sent)
         head_parts.append(head_c)
         prev_live = jnp.where(prev_keep, head_c, jnp.zeros_like(head_c))

time: 222 us -> 217 us (0.977)
  waiting for transfers between devices: 45.6 us -> 37.2 us
  starting transfers between devices: 19.3 us -> 23.9 us
    ppermute x3 -> x6, waiting for transfers between devices: 20 us -> 12.5 us  [the longest x3 12.5 us: per_device(): lax.ppermute(product_rev[:, :, :chunk], 'seq', [(d, 0)])]
    ppermute x3 -> x6, starting transfers between devices: 3.88 us -> 7.73 us  [the longest x3 3.86 us: per_device(): lax.ppermute(product_rev[:, :, chunk:], 'seq', [(d, 0)])]
    slice x4 -> x20, local copies, waits for them, and re-layouts: 6.28 us -> 4.08 us  [the longest x18 3.41 us: per_device(): part[:, :, rest_cols]]
  transfers between devices with their start and end apart: 11 -> 14, of which waited for: 2 -> 2; matrix products, arithmetic and copies ran while one was open for 61% -> 62% of each run, Pallas kernels for 0% -> 0%
where the time goes in v1:
time: 217 us
  matrix products  117 us (54%)
  waiting for transfers between devices  37.2 us (17%)
  starting transfers between devices  23.9 us (11%)
  local copies, waits for them, and re-layouts  14.6 us (7%)
  between operations  14.3 us (7%)
  other arithmetic  10.4 us (5%)
    conv_general_dilated x4, matrix products, correlate(): lax.conv_general_dilated(signal, kernel[:, None, :], (1,), 'VALID', dimen...  116 us
    reduce_scatter x4, waiting for transfers between devices, per_device(): reduced = lax.psum_scatter(blocks, 'seq', scatter_dimension=1, tiled=True)  24.6 us
    ppermute x4, starting transfers between devices, from_behind(): return lax.ppermute(block, axis, route)  15.4 us
    ppermute x3, waiting for transfers between devices, per_device(): lax.ppermute(product_rev[:, :, :chunk], 'seq', [(d, 0)])  12.5 us
    select_n x4, other arithmetic, per_device(): prev_live = jnp.where(prev_keep, head_c, jnp.zeros_like(head_c))  4.62 us
    rev x4, local copies, waits for them, and re-layouts, per_device(): blocks = partial_rev.reshape(requests, n_seq, own_tokens, chunk)[:, ::-1]  4.39 us
  transfers between devices with their start and end apart: 14, of which 2 were waited for; matrix products, arithmetic and copies ran while one was open for 62% of the time, Pallas kernels for 0%

profile of v1, /device:TPU:0, one launch (start us, length us, event | category | flops | bytes accessed | tf_op | source)
XLA Modules:
  0.0 216.9 jit_solution(1203116719111506165)
XLA Ops:
  7.2 1.5 multiply_convert_fusion.1
  10.5 1.3 collective-permute-start.2
  11.7 1.3 collective-permute-start.1
  13.0 1.3 collective-permute-start
  14.4 1.3 collective-permute-start.7
  15.7 1.4 fusion.18
  17.1 5.2 %collective-permute-start.3 = (bf16[2,256,512]{2,1,0:T(8,128)(2,1)}, bf16[2,256,512]{2,1,0:T(8,128)(2,1)}, u32[]{:S(2)}, u32[]{:S(2)}) collective-permute-start(bf16[2,256,512]{2,1,0:T(8,128)(2,1)} %get-tuple-element.50), channel_id=1, source_target_pairs={{0,4},{4,8},{8,12},{1,5},{5,9},{9,13},{2,6},{6,10},{10,14},{3,7},{... | collective-permute-start | bytes 1572872 | tf_op jit(solution)/shard_map/ppermute | solution.py:12
  24.7 12.5 %collective-permute-done.2 = bf16[2,64,512]{2,1,0:T(8,128)(2,1)S(1)} collective-permute-done((bf16[2,64,512]{2,1,0:T(8,128)(2,1)}, bf16[2,64,512]{2,1,0:T(8,128)(2,1)S(1)}, u32[]{:S(2)}, u32[]{:S(2)}) %collective-permute-start.2) | collective-permute-done | bytes 131104 | tf_op jit(solution)/shard_map/ppermute | solution.py:46
  37.2 1.3 collective-permute-start.6
  38.5 1.3 collective-permute-start.5
  39.8 4.6 %collective-permute-start.4 = (bf16[2,256,512]{2,1,0:T(8,128)(2,1)S(1)}, bf16[2,256,512]{2,1,0:T(8,128)(2,1)S(1)}, u32[]{:S(2)}, u32[]{:S(2)}) collective-permute-start(bf16[2,256,512]{2,1,0:T(8,128)(2,1)S(1)} %copy-done.10), channel_id=1, source_target_pairs={{0,4},{4,8},{8,12},{1,5},{5,9},{9,13},{2,6},{6,10},{10,14},{3,7},{... | collective-permute-start | bytes 1572872 | tf_op jit(solution)/shard_map/ppermute | solution.py:12
  44.4 3.5 %collective-permute-start.9 = (bf16[2,256,512]{2,1,0:T(8,128)(2,1)}, bf16[2,256,512]{2,1,0:T(8,128)(2,1)}, u32[]{:S(2)}, u32[]{:S(2)}) collective-permute-start(bf16[2,256,512]{2,1,0:T(8,128)(2,1)} %get-tuple-element.52), channel_id=1, source_target_pairs={{0,4},{4,8},{8,12},{1,5},{5,9},{9,13},{2,6},{6,10},{10,14},{3,7},{... | collective-permute-start | bytes 1572872 | tf_op jit(solution)/shard_map/ppermute | solution.py:12
  48.0 2.0 broadcast_select_fusion.4
  50.1 29.1 %fusion.7 = f32[2,256,512]{2,0,1:T(2,128)S(1)} fusion(bf16[2,511,512]{2,1,0:T(8,128)(2,1)S(1)} %pad_maximum_fusion.1, bf16[256,1,512]{2,0,1:T(8,128)(2,1)S(1)} %get-tuple-element.56), kind=kOutput, calls=%fused_computation.17 | convolution fusion | flops 134217728 | bytes 2357248 | tf_op jit(solution)/shard_map/conv_general_dilated | solution.py:17
  79.2 2.1 collective-permute-start.8
  85.6 1.3 broadcast_select_fusion.3
  87.0 29.1 %fusion.5 = f32[2,256,512]{2,0,1:T(2,128)S(1)} fusion(bf16[2,511,512]{2,1,0:T(8,128)(2,1)S(1)} %pad_maximum_fusion.2, bf16[256,1,512]{2,0,1:T(8,128)(2,1)S(1)} %copy-done.13), kind=kOutput, calls=%fused_computation.15 | convolution fusion | flops 134217728 | bytes 2357248 | tf_op jit(solution)/shard_map/conv_general_dilated | solution.py:17
  116.4 1.1 rev.16
  118.2 28.9 %fusion.3 = f32[2,256,512]{2,0,1:T(2,128)S(1)} fusion(bf16[2,511,512]{2,1,0:T(8,128)(2,1)S(1)} %pad_maximum_fusion.3, bf16[256,1,512]{2,0,1:T(8,128)(2,1)} %get-tuple-element.57), kind=kOutput, calls=%fused_computation.13 | convolution fusion | flops 134217728 | bytes 2357248 | tf_op jit(solution)/shard_map/conv_general_dilated | solution.py:17
  151.0 29.1 %fusion.1 = f32[2,256,512]{2,0,1:T(2,128)S(1)} fusion(bf16[2,511,512]{2,1,0:T(8,128)(2,1)S(1)} %pad_maximum_fusion.4, bf16[256,1,512]{2,0,1:T(8,128)(2,1)S(1)} %copy-done.11), kind=kOutput, calls=%fused_computation.11 | convolution fusion | flops 134217728 | bytes 2357248 | tf_op jit(solution)/shard_map/conv_general_dilated | solution.py:17
  180.4 1.1 rev.18
  181.5 1.6 pad_maximum_fusion
  183.2 24.6 %reduce-scatter.11.cloned.1.call-done = f32[2,1,64,512]{3,2,0,1:T(8,128)} async-done(((f32[2,4,64,512]{3,2,0,1:T(8,128)}), f32[2,1,64,512]{3,2,0,1:T(8,128)}) %reduce-scatter.11.cloned.1.call-update) | async-done | bytes 262160 | tf_op jit(solution)/shard_map/reduce_scatter | solution.py:79
  207.8 1.1 pad_maximum_fusion.5
  (96 shorter events, 15.1 us)
Async XLA Ops:
  7.2 8.5 %copy-start = (bf16[2,256,2048]{2,1,0:T(8,128)(2,1)S(1)}, bf16[2,256,2048]{2,1,0:T(8,128)(2,1)}, u32[]{:S(2)}) copy-start(bf16[2,256,2048]{2,1,0:T(8,128)(2,1)} %param.7) | copy-start | bytes 6291460
  7.2 110.7 %reduce-scatter.5.cloned.1.call-start = ((), (), s32[]{:S(2)}) async-start(), calls=%async_computation.4 | async-start | bytes 1310720 | tf_op jit(solution)/shard_map/reduce_scatter | solution.py:79
  10.5 26.7 %collective-permute-start.2 = (bf16[2,64,512]{2,1,0:T(8,128)(2,1)}, bf16[2,64,512]{2,1,0:T(8,128)(2,1)S(1)}, u32[]{:S(2)}, u32[]{:S(2)}) collective-permute-start(bf16[2,64,512]{2,1,0:T(8,128)(2,1)} %slice.110), channel_id=1, source_target_pairs={{4,0},{5,1},{6,2},{7,3},{20,16},{21,17},{22,18},{23,19}} | collective-permute-start | bytes 393224 | tf_op jit(solution)/shard_map/ppermute | solution.py:46
  11.7 26.7 %collective-permute-start.1 = (bf16[2,64,512]{2,1,0:T(8,128)(2,1)}, bf16[2,64,512]{2,1,0:T(8,128)(2,1)}, u32[]{:S(2)}, u32[]{:S(2)}) collective-permute-start(bf16[2,64,512]{2,1,0:T(8,128)(2,1)} %slice.110), channel_id=1, source_target_pairs={{8,0},{9,1},{10,2},{11,3},{24,16},{25,17},{26,18},{27,19}} | collective-permute-start | bytes 393224 | tf_op jit(solution)/shard_map/ppermute | solution.py:46
  13.0 26.7 %collective-permute-start = (bf16[2,64,512]{2,1,0:T(8,128)(2,1)}, bf16[2,64,512]{2,1,0:T(8,128)(2,1)}, u32[]{:S(2)}, u32[]{:S(2)}) collective-permute-start(bf16[2,64,512]{2,1,0:T(8,128)(2,1)} %slice.110), channel_id=1, source_target_pairs={{12,0},{13,1},{14,2},{15,3},{28,16},{29,17},{30,18},{31,19}} | collective-permute-start | bytes 393224 | tf_op jit(solution)/shard_map/ppermute | solution.py:46
  14.4 7.9 %copy-start.17 = (s32[2]{0:T(128)S(1)}, s32[2]{0:T(128)}, u32[]{:S(2)}) copy-start(s32[2]{0:T(128)} %param.9) | copy-start | bytes 28
  14.4 64.8 %collective-permute-start.7 = (bf16[2,64,1536]{2,1,0:T(8,128)(2,1)S(1)}, bf16[2,64,1536]{2,1,0:T(8,128)(2,1)S(1)}, u32[]{:S(2)}, u32[]{:S(2)}) collective-permute-start(bf16[2,64,1536]{2,1,0:T(8,128)(2,1)S(1)} %slice.112), channel_id=1, source_target_pairs={{12,0},{13,1},{14,2},{15,3},{28,16},{29,17},{30,18},{31,19}} | collective-permute-start | bytes 1179656 | tf_op jit(solution)/shard_map/ppermute | solution.py:49
  17.1 27.3 %collective-permute-start.3 = (bf16[2,256,512]{2,1,0:T(8,128)(2,1)}, bf16[2,256,512]{2,1,0:T(8,128)(2,1)}, u32[]{:S(2)}, u32[]{:S(2)}) collective-permute-start(bf16[2,256,512]{2,1,0:T(8,128)(2,1)} %get-tuple-element.50), channel_id=1, source_target_pairs={{0,4},{4,8},{8,12},{1,5},{5,9},{9,13},{2,6},{6,10},{10,14},{3,7},{... | collective-permute-start | bytes 1572872 | tf_op jit(solution)/shard_map/ppermute | solution.py:12
  23.8 16.0 %copy-start.10 = (bf16[2,256,512]{2,1,0:T(8,128)(2,1)S(1)}, bf16[2,256,512]{2,1,0:T(8,128)(2,1)}, u32[]{:S(2)}) copy-start(bf16[2,256,512]{2,1,0:T(8,128)(2,1)} %get-tuple-element.51) | copy-start | bytes 1572868
  37.2 44.2 %collective-permute-start.6 = (bf16[2,64,1536]{2,1,0:T(8,128)(2,1)S(1)}, bf16[2,64,1536]{2,1,0:T(8,128)(2,1)S(1)}, u32[]{:S(2)}, u32[]{:S(2)}) collective-permute-start(bf16[2,64,1536]{2,1,0:T(8,128)(2,1)S(1)} %slice.112), channel_id=1, source_target_pairs={{8,0},{9,1},{10,2},{11,3},{24,16},{25,17},{26,18},{27,19}} | collective-permute-start | bytes 1179656 | tf_op jit(solution)/shard_map/ppermute | solution.py:49
  38.5 42.9 %collective-permute-start.5 = (bf16[2,64,1536]{2,1,0:T(8,128)(2,1)S(1)}, bf16[2,64,1536]{2,1,0:T(8,128)(2,1)S(1)}, u32[]{:S(2)}, u32[]{:S(2)}) collective-permute-start(bf16[2,64,1536]{2,1,0:T(8,128)(2,1)S(1)} %slice.112), channel_id=1, source_target_pairs={{4,0},{5,1},{6,2},{7,3},{20,16},{21,17},{22,18},{23,19}} | collective-permute-start | bytes 1179656 | tf_op jit(solution)/shard_map/ppermute | solution.py:49
  39.8 41.6 %collective-permute-start.4 = (bf16[2,256,512]{2,1,0:T(8,128)(2,1)S(1)}, bf16[2,256,512]{2,1,0:T(8,128)(2,1)S(1)}, u32[]{:S(2)}, u32[]{:S(2)}) collective-permute-start(bf16[2,256,512]{2,1,0:T(8,128)(2,1)S(1)} %copy-done.10), channel_id=1, source_target_pairs={{0,4},{4,8},{8,12},{1,5},{5,9},{9,13},{2,6},{6,10},{10,14},{3,7},{... | collective-permute-start | bytes 1572872 | tf_op jit(solution)/shard_map/ppermute | solution.py:12
  44.4 102.6 %collective-permute-start.9 = (bf16[2,256,512]{2,1,0:T(8,128)(2,1)}, bf16[2,256,512]{2,1,0:T(8,128)(2,1)}, u32[]{:S(2)}, u32[]{:S(2)}) collective-permute-start(bf16[2,256,512]{2,1,0:T(8,128)(2,1)} %get-tuple-element.52), channel_id=1, source_target_pairs={{0,4},{4,8},{8,12},{1,5},{5,9},{9,13},{2,6},{6,10},{10,14},{3,7},{... | collective-permute-start | bytes 1572872 | tf_op jit(solution)/shard_map/ppermute | solution.py:12
  79.2 4.9 %copy-start.6 = (bf16[2,64,1536]{2,1,0:T(8,128)(2,1)}, bf16[2,64,1536]{2,1,0:T(8,128)(2,1)S(1)}, u32[]{:S(2)}) copy-start(bf16[2,64,1536]{2,1,0:T(8,128)(2,1)S(1)} %collective-permute-done.7) | copy-start | bytes 1179652
  79.2 36.9 %collective-permute-start.8 = (bf16[2,256,512]{2,1,0:T(8,128)(2,1)}, bf16[2,256,512]{2,1,0:T(8,128)(2,1)}, u32[]{:S(2)}, u32[]{:S(2)}) collective-permute-start(bf16[2,256,512]{2,1,0:T(8,128)(2,1)} %get-tuple-element.53), channel_id=1, source_target_pairs={{0,4},{4,8},{8,12},{1,5},{5,9},{9,13},{2,6},{6,10},{10,14},{3,7},{... | collective-permute-start | bytes 1572872 | tf_op jit(solution)/shard_map/ppermute | solution.py:12
  81.3 2.7 %copy-start.7 = (bf16[2,64,1536]{2,1,0:T(8,128)(2,1)}, bf16[2,64,1536]{2,1,0:T(8,128)(2,1)S(1)}, u32[]{:S(2)}) copy-start(bf16[2,64,1536]{2,1,0:T(8,128)(2,1)S(1)} %collective-permute-done.6) | copy-start | bytes 1179652
  81.4 2.7 %copy-start.8 = (bf16[2,64,1536]{2,1,0:T(8,128)(2,1)}, bf16[2,64,1536]{2,1,0:T(8,128)(2,1)S(1)}, u32[]{:S(2)}) copy-start(bf16[2,64,1536]{2,1,0:T(8,128)(2,1)S(1)} %collective-permute-done.5) | copy-start | bytes 1179652
  81.4 2.7 %copy-start.9 = (bf16[2,256,512]{2,1,0:T(8,128)(2,1)}, bf16[2,256,512]{2,1,0:T(8,128)(2,1)S(1)}, u32[]{:S(2)}) copy-start(bf16[2,256,512]{2,1,0:T(8,128)(2,1)S(1)} %collective-permute-done.4) | copy-start | bytes 1572868
  85.4 64.8 %reduce-scatter.7.cloned.1.call-start = ((), (), s32[]{:S(2)}) async-start(), calls=%async_computation.5 | async-start | bytes 1310720 | tf_op jit(solution)/shard_map/reduce_scatter | solution.py:79
  117.9 63.6 %reduce-scatter.9.cloned.1.call-start = ((), (), s32[]{:S(2)}) async-start(), calls=%async_computation.6 | async-start | bytes 1310720 | tf_op jit(solution)/shard_map/reduce_scatter | solution.py:79
  150.2 57.5 %reduce-scatter.11.cloned.1.call-start = ((), (), s32[]{:S(2)}) async-start(), calls=%async_computation.7 | async-start | bytes 1310720 | tf_op jit(solution)/shard_map/reduce_scatter | solution.py:79
  181.5 26.2 %copy-start.12 = (f32[2,1,64,512]{3,2,0,1:T(8,128)S(1)}, f32[2,1,64,512]{3,2,0,1:T(8,128)}, u32[]{:S(2)}) copy-start(f32[2,1,64,512]{3,2,0,1:T(8,128)} %reduce-scatter.5.cloned.1.call-done) | copy-start | bytes 786436
  181.5 26.2 %copy-start.14 = (f32[2,1,64,512]{3,2,0,1:T(8,128)S(1)}, f32[2,1,64,512]{3,2,0,1:T(8,128)}, u32[]{:S(2)}) copy-start(f32[2,1,64,512]{3,2,0,1:T(8,128)} %reduce-scatter.7.cloned.1.call-done) | copy-start | bytes 786436
  181.5 26.2 %copy-start.15 = (f32[2,1,64,512]{3,2,0,1:T(8,128)S(1)}, f32[2,1,64,512]{3,2,0,1:T(8,128)}, u32[]{:S(2)}) copy-start(f32[2,1,64,512]{3,2,0,1:T(8,128)} %reduce-scatter.9.cloned.1.call-done) | copy-start | bytes 786436
  (14 other events, 18.4 us)
Sparse Core Ops, SparseCore 0:
  85.5 26.0 reduce-scatter.4
  118.0 26.0 reduce-scatter.6
  150.3 26.0 reduce-scatter.8
  181.6 26.0 reduce-scatter.10

commit v2 on v1

--- a/solution.py
+++ b/solution.py
@@ -10,6 +10,15 @@
     devices = range(lax.axis_size(axis))
     route = [(i - distance, i) for i in devices if i - distance in devices]
     return lax.ppermute(block, axis, route)
+
+
+def send_reduce(blocks, position, n_seq):
+    total = lax.dynamic_index_in_dim(blocks, position, axis=1, keepdims=False)
+    for shift in range(1, n_seq):
+        piece = lax.dynamic_index_in_dim(blocks, (position + shift) % n_seq, axis=1, keepdims=False)
+        route = [(p, (p + shift) % n_seq) for p in range(n_seq)]
+        total = total + lax.ppermute(piece, "seq", route)
+    return total
 
 
 def correlate(signal, kernel):
@@ -56,11 +65,13 @@
 
     head_parts = []
     own_parts = []
+    scattered = []
+    partials = []
     for c in range(CHANNEL_CHUNKS):
         cols = slice(c * chunk, (c + 1) * chunk)
         sent = from_behind(history[:, :, cols], "seq", 1)
         if own_parts:
-            (sent, rest_each), _ = lax.optimization_barrier(((sent, rest_each), last_partial))
+            (sent, rest_each), _ = lax.optimization_barrier(((sent, rest_each), partials[max(c - 2, 0)]))
             rest_cols = slice((c - 1) * chunk, c * chunk)
             head_first = jnp.concatenate(
                 [part[:, :, rest_cols] for part in rest_each[::-1]], axis=1
@@ -71,13 +82,26 @@
         head_parts.append(head_c)
         prev_live = jnp.where(prev_keep, head_c, jnp.zeros_like(head_c))
         segment = jnp.concatenate([prev_live, live_rows[:, : tile_len - 1, cols]], axis=1)
+        if c >= 3 and (c - 2) % 2 == 1:
+            segment, _ = lax.optimization_barrier((segment, own_parts[c - 2]))
         partial_rev = correlate(segment, filter_taps[:, cols])
-        last_partial = partial_rev
+        partials.append(partial_rev)
         blocks = partial_rev.reshape(requests, n_seq, own_tokens, chunk)[:, ::-1]
-        if own_parts:
-            blocks, _ = lax.optimization_barrier((blocks, own_parts[-1]))
+        if c % 2 == 1 and c != CHANNEL_CHUNKS - 1:
+            own_parts.append(send_reduce(blocks, position, n_seq))
+            continue
+        if c == CHANNEL_CHUNKS - 1:
+            half = blocks.shape[3] // 2
+            linked = send_reduce(blocks[..., half:], position, n_seq)
+            blocks = blocks[..., :half]
+        if scattered:
+            blocks, _ = lax.optimization_barrier((blocks, scattered[-1]))
         reduced = lax.psum_scatter(blocks, "seq", scatter_dimension=1, tiled=True)
-        own_parts.append(reduced[:, 0])
+        scattered.append(reduced)
+        if c == CHANNEL_CHUNKS - 1:
+            own_parts.append(jnp.concatenate([reduced[:, 0], linked], axis=2))
+        else:
+            own_parts.append(reduced[:, 0])
     summed = jnp.concatenate(own_parts, axis=2)[:, ::-1]
     product_float = product_own.astype(jnp.float32)
     total = summed + skip_gain[None, None, :] * product_float

time: 217 us -> 228 us (1.051)
  waiting for transfers between devices: 37.2 us -> 19 us
  local copies, waits for them, and re-layouts: 14.6 us -> 28.9 us
  starting transfers between devices: 23.9 us -> 33.4 us
  other arithmetic: 10.4 us -> 14.3 us
    ppermute x3, waiting for transfers between devices: 12.5 us -> 0.01 us  [per_device(): lax.ppermute(product_rev[:, :, :chunk], 'seq', [(d, 0)])]
    ppermute x0 -> x6, starting transfers between devices: none -> 7.99 us  [send_reduce(): total = total + lax.ppermute(piece, 'seq', route)]
    rev x1, local copies, waits for them, and re-layouts: 0.45 us -> 6.83 us  [per_device(): summed = jnp.concatenate(own_parts, axis=2)[:, ::-1]]
    reduce_scatter x4 -> x3, waiting for transfers between devices: 24.6 us -> 18.9 us  [per_device(): reduced = lax.psum_scatter(blocks, 'seq', scatter_dimension=1, tiled=True)]
    unnamed x36 -> x48, local copies, waits for them, and re-layouts: 2.45 us -> 6.07 us
    dynamic_slice x0 -> x8, local copies, waits for them, and re-layouts: none -> 2.85 us  [the longest x6 2.29 us: send_reduce(): lax.dynamic_index_in_dim(blocks, (position + shift) % n_seq, axis=1, keep...]
    slice x18 -> x13, local copies, waits for them, and re-layouts: 3.41 us -> 4.76 us  [per_device(): part[:, :, rest_cols]]
    select_n x4 -> x3, other arithmetic: 4.62 us -> 4.6 us  [per_device(): prev_live = jnp.where(prev_keep, head_c, jnp.zeros_like(head_c))]
  transfers between devices with their start and end apart: 14 -> 19, of which waited for: 2 -> 2; matrix products, arithmetic and copies ran while one was open for 62% -> 63% of each run, Pallas kernels for 0% -> 0%
where the time goes in v2:
time: 228 us; the launch traced here: 227 us
  matrix products  117 us (51%)
  starting transfers between devices  33.4 us (15%)
  local copies, waits for them, and re-layouts  28.9 us (13%)
  waiting for transfers between devices  19 us (8%)
  between operations  14.4 us (6%)
  other arithmetic  14.3 us (6%)
    conv_general_dilated x4, matrix products, correlate(): lax.conv_general_dilated(signal, kernel[:, None, :], (1,), 'VALID', dimen...  117 us
    reduce_scatter x3, waiting for transfers between devices, per_device(): reduced = lax.psum_scatter(blocks, 'seq', scatter_dimension=1, tiled=True)  18.9 us
    ppermute x4, starting transfers between devices, from_behind(): return lax.ppermute(block, axis, route)  17.1 us
    ppermute x6, starting transfers between devices, send_reduce(): total = total + lax.ppermute(piece, 'seq', route)  7.99 us
    rev x1, local copies, waits for them, and re-layouts, per_device(): summed = jnp.concatenate(own_parts, axis=2)[:, ::-1]  6.83 us
    unnamed x48, local copies, waits for them, and re-layouts  6.07 us
    slice x13, local copies, waits for them, and re-layouts, per_device(): part[:, :, rest_cols]  4.76 us
    select_n x3, other arithmetic, per_device(): prev_live = jnp.where(prev_keep, head_c, jnp.zeros_like(head_c))  4.6 us
  transfers between devices with their start and end apart: 19, of which 2 were waited for; matrix products, arithmetic and copies ran while one was open for 63% of the time, Pallas kernels for 0%

profile of v2, /device:TPU:0, one launch (start us, length us, event | category | flops | bytes accessed | tf_op | source)
XLA Modules:
  0.0 227.4 jit_solution(15242753267557323164)
XLA Ops:
  7.2 1.5 multiply_convert_fusion.1
  9.8 1.3 collective-permute-start
  13.7 1.4 fusion.23
  15.1 5.6 %collective-permute-start.3 = (bf16[2,256,512]{2,1,0:T(8,128)(2,1)}, bf16[2,256,512]{2,1,0:T(8,128)(2,1)S(1)}, u32[]{:S(2)}, u32[]{:S(2)}) collective-permute-start(bf16[2,256,512]{2,1,0:T(8,128)(2,1)} %get-tuple-element.50), channel_id=1, source_target_pairs={{0,4},{4,8},{8,12},{1,5},{5,9},{9,13},{2,6},{6,10},{10,14},{3,7},{... | collective-permute-start | bytes 1572872 | tf_op jit(solution)/shard_map/ppermute | solution.py:12
  22.2 1.5 broadcast_select_fusion
  23.7 1.8 fusion.24
  29.1 3.4 %collective-permute-start.4 = (bf16[2,256,512]{2,1,0:T(8,128)(2,1)S(1)}, bf16[2,256,512]{2,1,0:T(8,128)(2,1)S(1)}, u32[]{:S(2)}, u32[]{:S(2)}) collective-permute-start(bf16[2,256,512]{2,1,0:T(8,128)(2,1)S(1)} %copy-done.16), channel_id=1, source_target_pairs={{0,4},{4,8},{8,12},{1,5},{5,9},{9,13},{2,6},{6,10},{10,14},{3,7},{... | collective-permute-start | bytes 1572872 | tf_op jit(solution)/shard_map/ppermute | solution.py:12
  32.5 4.1 %collective-permute-start.11 = (bf16[2,256,512]{2,1,0:T(8,128)(2,1)S(1)}, bf16[2,256,512]{2,1,0:T(8,128)(2,1)S(1)}, u32[]{:S(2)}, u32[]{:S(2)}) collective-permute-start(bf16[2,256,512]{2,1,0:T(8,128)(2,1)S(1)} %copy-done.15), channel_id=1, source_target_pairs={{0,4},{4,8},{8,12},{1,5},{5,9},{9,13},{2,6},{6,10},{10,14},{3,7},{... | collective-permute-start | bytes 1572872 | tf_op jit(solution)/shard_map/ppermute | solution.py:12
  36.6 2.0 broadcast_select_fusion.4
  38.7 29.8 %fusion.7 = f32[2,256,512]{2,0,1:T(2,128)} fusion(bf16[2,511,512]{2,1,0:T(8,128)(2,1)S(1)} %pad_maximum_fusion.1, bf16[256,1,512]{2,0,1:T(8,128)(2,1)S(1)} %get-tuple-element.60), kind=kOutput, calls=%fused_computation.16 | convolution fusion | flops 134217728 | bytes 2357248 | tf_op jit(solution)/shard_map/conv_general_dilated | solution.py:26
  68.5 4.0 %collective-permute-start.12 = (bf16[2,256,512]{2,1,0:T(8,128)(2,1)S(1)}, bf16[2,256,512]{2,1,0:T(8,128)(2,1)S(1)}, u32[]{:S(2)}, u32[]{:S(2)}) collective-permute-start(bf16[2,256,512]{2,1,0:T(8,128)(2,1)S(1)} %copy-done.14), channel_id=1, source_target_pairs={{0,4},{4,8},{8,12},{1,5},{5,9},{9,13},{2,6},{6,10},{10,14},{3,7},{... | collective-permute-start | bytes 1572872 | tf_op jit(solution)/shard_map/ppermute | solution.py:12
  73.7 29.1 %fusion.5 = f32[2,256,512]{2,0,1:T(2,128)S(1)} fusion(bf16[2,511,512]{2,1,0:T(8,128)(2,1)S(1)} %pad_maximum_fusion.2, bf16[256,1,512]{2,0,1:T(8,128)(2,1)S(1)} %get-tuple-element.59), kind=kOutput, calls=%fused_computation.14 | convolution fusion | flops 134217728 | bytes 2357248 | tf_op jit(solution)/shard_map/conv_general_dilated | solution.py:26
  109.9 2.0 collective-permute-start.8
  114.9 1.6 broadcast_select_fusion.1
  117.5 29.1 %fusion.3 = f32[2,256,512]{2,0,1:T(2,128)S(1)} fusion(bf16[2,511,512]{2,1,0:T(8,128)(2,1)S(1)} %pad_maximum_fusion.3, bf16[256,1,512]{2,0,1:T(8,128)(2,1)S(1)} %copy-done.19), kind=kOutput, calls=%fused_computation.12 | convolution fusion | flops 134217728 | bytes 2357248 | tf_op jit(solution)/shard_map/conv_general_dilated | solution.py:26
  149.4 1.7 bitcast_dynamic-update-slice_fusion.1
  151.2 2.0 constant_dynamic-update-slice_fusion
  153.5 29.1 %fusion.1 = f32[2,256,512]{2,0,1:T(2,128)S(1)} fusion(bf16[2,511,512]{2,1,0:T(8,128)(2,1)S(1)} %copy-done.7, bf16[256,1,512]{2,0,1:T(8,128)(2,1)S(1)} %copy-done.18), kind=kOutput, calls=%fused_computation.10 | convolution fusion | flops 134217728 | bytes 2357248 | tf_op jit(solution)/shard_map/conv_general_dilated | solution.py:26
  184.0 1.6 pad_maximum_fusion
  186.1 2.2 collective-permute-start.13
  189.3 2.3 %collective-permute-start.15 = (f32[2,64,256]{2,1,0:T(8,128)S(1)}, f32[2,64,256]{2,1,0:T(8,128)S(1)}, u32[]{:S(2)}, u32[]{:S(2)}) collective-permute-start(f32[2,64,256]{2,1,0:T(8,128)S(1)} %bitcast.63), channel_id=1, source_target_pairs={{0,12},{4,0},{8,4},{12,8},{1,13},{5,1},{9,5},{13,9},{2,14},{6,2},{... | collective-permute-start | bytes 393224 | tf_op jit(solution)/shard_map/ppermute | solution.py:20
  192.3 18.4 %reduce-scatter.8.cloned.1.call-done = f32[2,1,64,256]{3,2,0,1:T(8,128)} async-done(((f32[2,4,64,256]{3,2,0,1:T(8,128)}), f32[2,1,64,256]{3,2,0,1:T(8,128)}) %reduce-scatter.8.cloned.1.call-update) | async-done | bytes 131088 | tf_op jit(solution)/shard_map/reduce_scatter | solution.py:99
  210.8 1.6 bitcast_dynamic-update-slice_fusion.2
  213.1 6.8 %rev.16 = f32[2,64,2048]{2,1,0:T(8,128)S(1)} reverse(f32[2,64,2048]{2,1,0:T(8,128)} %fusion.17), dimensions={1} | reverse | bytes 2097152 | tf_op jit(solution)/shard_map/rev | solution.py:105
  (120 shorter events, 29.1 us)
Async XLA Ops:
  7.2 142.3 %reduce-scatter.4.cloned.1.call-start = ((), (), s32[]{:S(2)}) async-start(), calls=%async_computation.3 | async-start | bytes 1310720 | tf_op jit(solution)/shard_map/reduce_scatter | solution.py:99
  9.8 16.7 %collective-permute-start = (bf16[2,64,512]{2,1,0:T(8,128)(2,1)S(1)}, bf16[2,64,512]{2,1,0:T(8,128)(2,1)}, u32[]{:S(2)}, u32[]{:S(2)}) collective-permute-start(bf16[2,64,512]{2,1,0:T(8,128)(2,1)S(1)} %slice.126), channel_id=1, source_target_pairs={{12,0},{13,1},{14,2},{15,3},{28,16},{29,17},{30,18},{31,19}} | collective-permute-start | bytes 393224 | tf_op jit(solution)/shard_map/ppermute | solution.py:55
  11.1 16.7 %collective-permute-start.1 = (bf16[2,64,512]{2,1,0:T(8,128)(2,1)S(1)}, bf16[2,64,512]{2,1,0:T(8,128)(2,1)}, u32[]{:S(2)}, u32[]{:S(2)}) collective-permute-start(bf16[2,64,512]{2,1,0:T(8,128)(2,1)S(1)} %slice.126), channel_id=1, source_target_pairs={{8,0},{9,1},{10,2},{11,3},{24,16},{25,17},{26,18},{27,19}} | collective-permute-start | bytes 393224 | tf_op jit(solution)/shard_map/ppermute | solution.py:55
  12.4 16.7 %collective-permute-start.2 = (bf16[2,64,512]{2,1,0:T(8,128)(2,1)S(1)}, bf16[2,64,512]{2,1,0:T(8,128)(2,1)}, u32[]{:S(2)}, u32[]{:S(2)}) collective-permute-start(bf16[2,64,512]{2,1,0:T(8,128)(2,1)S(1)} %slice.126), channel_id=1, source_target_pairs={{4,0},{5,1},{6,2},{7,3},{20,16},{21,17},{22,18},{23,19}} | collective-permute-start | bytes 393224 | tf_op jit(solution)/shard_map/ppermute | solution.py:55
  15.1 17.4 %collective-permute-start.3 = (bf16[2,256,512]{2,1,0:T(8,128)(2,1)}, bf16[2,256,512]{2,1,0:T(8,128)(2,1)S(1)}, u32[]{:S(2)}, u32[]{:S(2)}) collective-permute-start(bf16[2,256,512]{2,1,0:T(8,128)(2,1)} %get-tuple-element.50), channel_id=1, source_target_pairs={{0,4},{4,8},{8,12},{1,5},{5,9},{9,13},{2,6},{6,10},{10,14},{3,7},{... | collective-permute-start | bytes 1572872 | tf_op jit(solution)/shard_map/ppermute | solution.py:12
  20.8 47.8 %collective-permute-start.5 = (bf16[2,64,1536]{2,1,0:T(8,128)(2,1)S(1)}, bf16[2,64,1536]{2,1,0:T(8,128)(2,1)S(1)}, u32[]{:S(2)}, u32[]{:S(2)}) collective-permute-start(bf16[2,64,1536]{2,1,0:T(8,128)(2,1)S(1)} %slice.128), channel_id=1, source_target_pairs={{4,0},{5,1},{6,2},{7,3},{20,16},{21,17},{22,18},{23,19}} | collective-permute-start | bytes 1179656 | tf_op jit(solution)/shard_map/ppermute | solution.py:58
  26.5 46.1 %collective-permute-start.6 = (bf16[2,64,1536]{2,1,0:T(8,128)(2,1)S(1)}, bf16[2,64,1536]{2,1,0:T(8,128)(2,1)S(1)}, u32[]{:S(2)}, u32[]{:S(2)}) collective-permute-start(bf16[2,64,1536]{2,1,0:T(8,128)(2,1)S(1)} %slice.128), channel_id=1, source_target_pairs={{8,0},{9,1},{10,2},{11,3},{24,16},{25,17},{26,18},{27,19}} | collective-permute-start | bytes 1179656 | tf_op jit(solution)/shard_map/ppermute | solution.py:58
  27.8 44.8 %collective-permute-start.7 = (bf16[2,64,1536]{2,1,0:T(8,128)(2,1)S(1)}, bf16[2,64,1536]{2,1,0:T(8,128)(2,1)S(1)}, u32[]{:S(2)}, u32[]{:S(2)}) collective-permute-start(bf16[2,64,1536]{2,1,0:T(8,128)(2,1)S(1)} %slice.128), channel_id=1, source_target_pairs={{12,0},{13,1},{14,2},{15,3},{28,16},{29,17},{30,18},{31,19}} | collective-permute-start | bytes 1179656 | tf_op jit(solution)/shard_map/ppermute | solution.py:58
  29.1 43.5 %collective-permute-start.4 = (bf16[2,256,512]{2,1,0:T(8,128)(2,1)S(1)}, bf16[2,256,512]{2,1,0:T(8,128)(2,1)S(1)}, u32[]{:S(2)}, u32[]{:S(2)}) collective-permute-start(bf16[2,256,512]{2,1,0:T(8,128)(2,1)S(1)} %copy-done.16), channel_id=1, source_target_pairs={{0,4},{4,8},{8,12},{1,5},{5,9},{9,13},{2,6},{6,10},{10,14},{3,7},{... | collective-permute-start | bytes 1572872 | tf_op jit(solution)/shard_map/ppermute | solution.py:12
  32.5 70.4 %collective-permute-start.11 = (bf16[2,256,512]{2,1,0:T(8,128)(2,1)S(1)}, bf16[2,256,512]{2,1,0:T(8,128)(2,1)S(1)}, u32[]{:S(2)}, u32[]{:S(2)}) collective-permute-start(bf16[2,256,512]{2,1,0:T(8,128)(2,1)S(1)} %copy-done.15), channel_id=1, source_target_pairs={{0,4},{4,8},{8,12},{1,5},{5,9},{9,13},{2,6},{6,10},{10,14},{3,7},{... | collective-permute-start | bytes 1572872 | tf_op jit(solution)/shard_map/ppermute | solution.py:12
  38.7 29.8 %copy-start.14 = (bf16[2,256,512]{2,1,0:T(8,128)(2,1)S(1)}, bf16[2,256,512]{2,1,0:T(8,128)(2,1)}, u32[]{:S(2)}) copy-start(bf16[2,256,512]{2,1,0:T(8,128)(2,1)} %get-tuple-element.48) | copy-start | bytes 1572868
  68.5 36.4 %collective-permute-start.12 = (bf16[2,256,512]{2,1,0:T(8,128)(2,1)S(1)}, bf16[2,256,512]{2,1,0:T(8,128)(2,1)S(1)}, u32[]{:S(2)}, u32[]{:S(2)}) collective-permute-start(bf16[2,256,512]{2,1,0:T(8,128)(2,1)S(1)} %copy-done.14), channel_id=1, source_target_pairs={{0,4},{4,8},{8,12},{1,5},{5,9},{9,13},{2,6},{6,10},{10,14},{3,7},{... | collective-permute-start | bytes 1572872 | tf_op jit(solution)/shard_map/ppermute | solution.py:12
  72.6 32.4 %copy-start.13 = (bf16[2,64,1536]{2,1,0:T(8,128)(2,1)}, bf16[2,64,1536]{2,1,0:T(8,128)(2,1)S(1)}, u32[]{:S(2)}) copy-start(bf16[2,64,1536]{2,1,0:T(8,128)(2,1)S(1)} %collective-permute-done.7) | copy-start | bytes 1179652
  109.1 42.0 %collective-permute-start.10 = (f32[2,64,512]{2,1,0:T(8,128)}, f32[2,64,512]{2,1,0:T(8,128)}, u32[]{:S(2)}, u32[]{:S(2)}) collective-permute-start(f32[2,64,512]{2,1,0:T(8,128)} %bitcast.51), channel_id=1, source_target_pairs={{0,12},{4,0},{8,4},{12,8},{1,13},{5,1},{9,5},{13,9},{2,14},{6,2},{... | collective-permute-start | bytes 786440 | tf_op jit(solution)/shard_map/ppermute | solution.py:20
  109.9 41.3 %collective-permute-start.8 = (f32[2,64,512]{2,1,0:T(8,128)}, f32[2,64,512]{2,1,0:T(8,128)}, u32[]{:S(2)}, u32[]{:S(2)}) collective-permute-start(f32[2,64,512]{2,1,0:T(8,128)} %bitcast.53), channel_id=1, source_target_pairs={{0,4},{4,8},{8,12},{12,0},{1,5},{5,9},{9,13},{13,1},{2,6},{6,10},{... | collective-permute-start | bytes 786440 | tf_op jit(solution)/shard_map/ppermute | solution.py:20
  112.7 38.5 %collective-permute-start.9 = (f32[2,64,512]{2,1,0:T(8,128)}, f32[2,64,512]{2,1,0:T(8,128)}, u32[]{:S(2)}, u32[]{:S(2)}) collective-permute-start(f32[2,64,512]{2,1,0:T(8,128)} %bitcast.52), channel_id=1, source_target_pairs={{0,8},{4,12},{8,0},{12,4},{1,9},{5,13},{9,1},{13,5},{2,10},{6,14},... | collective-permute-start | bytes 786440 | tf_op jit(solution)/shard_map/ppermute | solution.py:20
  114.5 69.5 %reduce-scatter.6.cloned.1.call-start = ((), (), s32[]{:S(2)}) async-start(), calls=%async_computation.4 | async-start | bytes 1310720 | tf_op jit(solution)/shard_map/reduce_scatter | solution.py:99
  153.2 57.6 %reduce-scatter.8.cloned.1.call-start = ((), (), s32[]{:S(2)}) async-start(), calls=%async_computation.5 | async-start | bytes 655360 | tf_op jit(solution)/shard_map/reduce_scatter | solution.py:99
  186.0 33.8 %copy-start.2 = (bf16[2,64,2048]{2,1,0:T(8,128)(2,1)S(1)}, bf16[2,64,2048]{2,1,0:T(8,128)(2,1)}, u32[]{:S(2)}) copy-start(bf16[2,64,2048]{2,1,0:T(8,128)(2,1)} %copy-done.1) | copy-start | bytes 1572868
  186.1 33.8 %copy-start.8 = (bf16[2,64,2048]{2,1,0:T(8,128)(2,1)S(1)}, bf16[2,64,2048]{2,1,0:T(8,128)(2,1)}, u32[]{:S(2)}) copy-start(bf16[2,64,2048]{2,1,0:T(8,128)(2,1)} %param.12) | copy-start | bytes 1572868
  186.1 33.8 %copy-start.20 = (f32[2048]{0:T(1024)S(1)}, f32[2048]{0:T(1024)}, u32[]{:S(2)}) copy-start(f32[2048]{0:T(1024)} %param.13) | copy-start | bytes 24580
  186.1 26.3 %collective-permute-start.13 = (f32[2,64,256]{2,1,0:T(8,128)S(1)}, f32[2,64,256]{2,1,0:T(8,128)S(1)}, u32[]{:S(2)}, u32[]{:S(2)}) collective-permute-start(f32[2,64,256]{2,1,0:T(8,128)S(1)} %bitcast.61), channel_id=1, source_target_pairs={{0,4},{4,8},{8,12},{12,0},{1,5},{5,9},{9,13},{13,1},{2,6},{6,10},{... | collective-permute-start | bytes 393224 | tf_op jit(solution)/shard_map/ppermute | solution.py:20
  188.3 24.0 %collective-permute-start.14 = (f32[2,64,256]{2,1,0:T(8,128)S(1)}, f32[2,64,256]{2,1,0:T(8,128)S(1)}, u32[]{:S(2)}, u32[]{:S(2)}) collective-permute-start(f32[2,64,256]{2,1,0:T(8,128)S(1)} %bitcast.62), channel_id=1, source_target_pairs={{0,8},{4,12},{8,0},{12,4},{1,9},{5,13},{9,1},{13,5},{2,10},{6,14},... | collective-permute-start | bytes 393224 | tf_op jit(solution)/shard_map/ppermute | solution.py:20
  189.3 23.0 %collective-permute-start.15 = (f32[2,64,256]{2,1,0:T(8,128)S(1)}, f32[2,64,256]{2,1,0:T(8,128)S(1)}, u32[]{:S(2)}, u32[]{:S(2)}) collective-permute-start(f32[2,64,256]{2,1,0:T(8,128)S(1)} %bitcast.63), channel_id=1, source_target_pairs={{0,12},{4,0},{8,4},{12,8},{1,13},{5,1},{9,5},{13,9},{2,14},{6,2},{... | collective-permute-start | bytes 393224 | tf_op jit(solution)/shard_map/ppermute | solution.py:20
  (18 other events, 68.8 us)
Sparse Core Ops, SparseCore 0:
  114.6 34.8 reduce-scatter.3
  153.3 28.0 reduce-scatter.5
  184.1 26.5 reduce-scatter.7

commit v3 on v1

--- a/solution.py
+++ b/solution.py
@@ -78,7 +78,13 @@
             blocks, _ = lax.optimization_barrier((blocks, own_parts[-1]))
         reduced = lax.psum_scatter(blocks, "seq", scatter_dimension=1, tiled=True)
         own_parts.append(reduced[:, 0])
-    summed = jnp.concatenate(own_parts, axis=2)[:, ::-1]
+    summed = jnp.einsum(
+        "ik,rkc->ric",
+        exchange.astype(jnp.float32),
+        jnp.concatenate(own_parts, axis=2),
+        precision=lax.Precision.HIGHEST,
+        preferred_element_type=jnp.float32,
+    )
     product_float = product_own.astype(jnp.float32)
     total = summed + skip_gain[None, None, :] * product_float
     mixed = (outer_gate.astype(jnp.float32) * total).astype(jnp.bfloat16)

time: 217 us -> 218 us (level)
    dot_general x0 -> x1, matrix products: none -> 2.75 us  [per_device(): jnp.einsum('ik,rkc->ric', exchange.astype(jnp.float32), jnp.concatenate(o...]
where the time goes in v3:
time: 218 us; the launch traced here: 217 us
  matrix products  119 us (55%)
  waiting for transfers between devices  38 us (17%)
  starting transfers between devices  23.1 us (11%)
  between operations  14.2 us (7%)
  local copies, waits for them, and re-layouts  14.1 us (6%)
  other arithmetic  8.29 us (4%)
    conv_general_dilated x4, matrix products, correlate(): lax.conv_general_dilated(signal, kernel[:, None, :], (1,), 'VALID', dimen...  116 us
    reduce_scatter x4, waiting for transfers between devices, per_device(): reduced = lax.psum_scatter(blocks, 'seq', scatter_dimension=1, tiled=True)  24.6 us
    ppermute x4, starting transfers between devices, from_behind(): return lax.ppermute(block, axis, route)  14.6 us
    ppermute x3, waiting for transfers between devices, per_device(): lax.ppermute(product_rev[:, :, :chunk], 'seq', [(d, 0)])  13.3 us
    select_n x4, other arithmetic, per_device(): prev_live = jnp.where(prev_keep, head_c, jnp.zeros_like(head_c))  4.61 us
    rev x4, local copies, waits for them, and re-layouts, per_device(): blocks = partial_rev.reshape(requests, n_seq, own_tokens, chunk)[:, ::-1]  4.41 us
  transfers between devices with their start and end apart: 14, of which 2 were waited for; matrix products, arithmetic and copies ran while one was open for 62% of the time, Pallas kernels for 0%

profile of v3, /device:TPU:0, one launch (start us, length us, event | category | flops | bytes accessed | tf_op | source)
XLA Modules:
  0.0 217.1 jit_solution(5580648415839998241)
XLA Ops:
  7.2 1.5 multiply_convert_fusion
  10.5 1.3 collective-permute-start.2
  11.7 1.3 collective-permute-start.1
  13.0 1.3 collective-permute-start
  14.4 1.3 collective-permute-start.7
  15.7 1.4 fusion.32
  17.1 4.4 %collective-permute-start.3 = (bf16[2,256,512]{2,1,0:T(8,128)(2,1)}, bf16[2,256,512]{2,1,0:T(8,128)(2,1)S(1)}, u32[]{:S(2)}, u32[]{:S(2)}) collective-permute-start(bf16[2,256,512]{2,1,0:T(8,128)(2,1)} %get-tuple-element.50), channel_id=1, source_target_pairs={{0,4},{4,8},{8,12},{1,5},{5,9},{9,13},{2,6},{6,10},{10,14},{3,7},{... | collective-permute-start | bytes 1572872 | tf_op jit(solution)/shard_map/ppermute | solution.py:12
  23.9 13.3 %collective-permute-done.2 = bf16[2,64,512]{2,1,0:T(8,128)(2,1)S(1)} collective-permute-done((bf16[2,64,512]{2,1,0:T(8,128)(2,1)}, bf16[2,64,512]{2,1,0:T(8,128)(2,1)S(1)}, u32[]{:S(2)}, u32[]{:S(2)}) %collective-permute-start.2) | collective-permute-done | bytes 131104 | tf_op jit(solution)/shard_map/ppermute | solution.py:46
  37.2 1.3 collective-permute-start.6
  38.5 1.3 collective-permute-start.5
  39.8 4.6 %collective-permute-start.4 = (bf16[2,256,512]{2,1,0:T(8,128)(2,1)S(1)}, bf16[2,256,512]{2,1,0:T(8,128)(2,1)S(1)}, u32[]{:S(2)}, u32[]{:S(2)}) collective-permute-start(bf16[2,256,512]{2,1,0:T(8,128)(2,1)S(1)} %copy-done.9), channel_id=1, source_target_pairs={{0,4},{4,8},{8,12},{1,5},{5,9},{9,13},{2,6},{6,10},{10,14},{3,7},{... | collective-permute-start | bytes 1572872 | tf_op jit(solution)/shard_map/ppermute | solution.py:12
  44.4 3.5 %collective-permute-start.9 = (bf16[2,256,512]{2,1,0:T(8,128)(2,1)}, bf16[2,256,512]{2,1,0:T(8,128)(2,1)}, u32[]{:S(2)}, u32[]{:S(2)}) collective-permute-start(bf16[2,256,512]{2,1,0:T(8,128)(2,1)} %get-tuple-element.52), channel_id=1, source_target_pairs={{0,4},{4,8},{8,12},{1,5},{5,9},{9,13},{2,6},{6,10},{10,14},{3,7},{... | collective-permute-start | bytes 1572872 | tf_op jit(solution)/shard_map/ppermute | solution.py:12
  48.0 2.0 broadcast_select_fusion.4
  50.1 29.1 %fusion.17 = f32[2,256,512]{2,0,1:T(2,128)S(1)} fusion(bf16[2,511,512]{2,1,0:T(8,128)(2,1)S(1)} %pad_maximum_fusion.1, bf16[256,1,512]{2,0,1:T(8,128)(2,1)S(1)} %get-tuple-element.56), kind=kOutput, calls=%fused_computation.26 | convolution fusion | flops 134217728 | bytes 2357248 | tf_op jit(solution)/shard_map/conv_general_dilated | solution.py:17
  79.2 2.1 collective-permute-start.8
  85.6 1.3 broadcast_select_fusion.3
  87.0 29.1 %fusion.15 = f32[2,256,512]{2,0,1:T(2,128)S(1)} fusion(bf16[2,511,512]{2,1,0:T(8,128)(2,1)S(1)} %pad_maximum_fusion.2, bf16[256,1,512]{2,0,1:T(8,128)(2,1)S(1)} %copy-done.11), kind=kOutput, calls=%fused_computation.24 | convolution fusion | flops 134217728 | bytes 2357248 | tf_op jit(solution)/shard_map/conv_general_dilated | solution.py:17
  116.4 1.1 rev.13
  118.2 28.9 %fusion.13 = f32[2,256,512]{2,0,1:T(2,128)S(1)} fusion(bf16[2,511,512]{2,1,0:T(8,128)(2,1)S(1)} %pad_maximum_fusion.3, bf16[256,1,512]{2,0,1:T(8,128)(2,1)} %get-tuple-element.57), kind=kOutput, calls=%fused_computation.22 | convolution fusion | flops 134217728 | bytes 2357248 | tf_op jit(solution)/shard_map/conv_general_dilated | solution.py:17
  151.0 29.1 %fusion.11 = f32[2,256,512]{2,0,1:T(2,128)S(1)} fusion(bf16[2,511,512]{2,1,0:T(8,128)(2,1)S(1)} %pad_maximum_fusion.4, bf16[256,1,512]{2,0,1:T(8,128)(2,1)S(1)} %copy-done.10), kind=kOutput, calls=%fused_computation.20 | convolution fusion | flops 134217728 | bytes 2357248 | tf_op jit(solution)/shard_map/conv_general_dilated | solution.py:17
  180.4 1.1 rev.15
  181.6 1.6 pad_maximum_fusion
  183.2 24.6 %reduce-scatter.11.cloned.1.call-done = f32[2,1,64,512]{3,2,0,1:T(8,128)} async-done(((f32[2,4,64,512]{3,2,0,1:T(8,128)}), f32[2,1,64,512]{3,2,0,1:T(8,128)}) %reduce-scatter.11.cloned.1.call-update) | async-done | bytes 262160 | tf_op jit(solution)/shard_map/reduce_scatter | solution.py:79
  207.8 2.8 %fusion.2 = bf16[2,64,2048]{2,1,0:T(8,128)(2,1)} fusion(f32[2,64,512]{2,1,0:T(8,128)} %bitcast.38, f32[2,64,512]{2,1,0:T(8,128)} %bitcast.37, f32[2,64,512]{2,1,0:T(8,128)} %bitcast.36, f32[2,64,512]{2,1,0:T(8,128)S(1)} %bitcast.35, bf16[2,64,2048]{2,1,0:T(8,128)(2,1)S(1)} %copy-done.2, bf16[2,64,2048]{2,1,0:T(8,128)(2,1)S(1)} %copy-done.13, ...), kind=kOutput, calls=%fused_computation.3 | convolution fusion | flops 203694080 | bytes 2629632 | tf_op jit(solution)/shard_map/ik,rkc->ric/dot_general | solution.py:81
  (90 shorter events, 13.6 us)
Async XLA Ops:
  7.2 8.5 %copy-start = (bf16[2,256,2048]{2,1,0:T(8,128)(2,1)S(1)}, bf16[2,256,2048]{2,1,0:T(8,128)(2,1)}, u32[]{:S(2)}) copy-start(bf16[2,256,2048]{2,1,0:T(8,128)(2,1)} %param.7) | copy-start | bytes 6291460
  7.2 110.7 %reduce-scatter.5.cloned.1.call-start = ((), (), s32[]{:S(2)}) async-start(), calls=%async_computation.4 | async-start | bytes 1310720 | tf_op jit(solution)/shard_map/reduce_scatter | solution.py:79
  10.5 26.7 %collective-permute-start.2 = (bf16[2,64,512]{2,1,0:T(8,128)(2,1)}, bf16[2,64,512]{2,1,0:T(8,128)(2,1)S(1)}, u32[]{:S(2)}, u32[]{:S(2)}) collective-permute-start(bf16[2,64,512]{2,1,0:T(8,128)(2,1)} %slice.110), channel_id=1, source_target_pairs={{4,0},{5,1},{6,2},{7,3},{20,16},{21,17},{22,18},{23,19}} | collective-permute-start | bytes 393224 | tf_op jit(solution)/shard_map/ppermute | solution.py:46
  11.7 26.7 %collective-permute-start.1 = (bf16[2,64,512]{2,1,0:T(8,128)(2,1)}, bf16[2,64,512]{2,1,0:T(8,128)(2,1)}, u32[]{:S(2)}, u32[]{:S(2)}) collective-permute-start(bf16[2,64,512]{2,1,0:T(8,128)(2,1)} %slice.110), channel_id=1, source_target_pairs={{8,0},{9,1},{10,2},{11,3},{24,16},{25,17},{26,18},{27,19}} | collective-permute-start | bytes 393224 | tf_op jit(solution)/shard_map/ppermute | solution.py:46
  13.0 26.7 %collective-permute-start = (bf16[2,64,512]{2,1,0:T(8,128)(2,1)}, bf16[2,64,512]{2,1,0:T(8,128)(2,1)}, u32[]{:S(2)}, u32[]{:S(2)}) collective-permute-start(bf16[2,64,512]{2,1,0:T(8,128)(2,1)} %slice.110), channel_id=1, source_target_pairs={{12,0},{13,1},{14,2},{15,3},{28,16},{29,17},{30,18},{31,19}} | collective-permute-start | bytes 393224 | tf_op jit(solution)/shard_map/ppermute | solution.py:46
  14.4 7.1 %copy-start.12 = (s32[2]{0:T(128)S(1)}, s32[2]{0:T(128)}, u32[]{:S(2)}) copy-start(s32[2]{0:T(128)} %param.9) | copy-start | bytes 28
  14.4 64.8 %collective-permute-start.7 = (bf16[2,64,1536]{2,1,0:T(8,128)(2,1)S(1)}, bf16[2,64,1536]{2,1,0:T(8,128)(2,1)S(1)}, u32[]{:S(2)}, u32[]{:S(2)}) collective-permute-start(bf16[2,64,1536]{2,1,0:T(8,128)(2,1)S(1)} %slice.112), channel_id=1, source_target_pairs={{12,0},{13,1},{14,2},{15,3},{28,16},{29,17},{30,18},{31,19}} | collective-permute-start | bytes 1179656 | tf_op jit(solution)/shard_map/ppermute | solution.py:49
  17.1 27.4 %collective-permute-start.3 = (bf16[2,256,512]{2,1,0:T(8,128)(2,1)}, bf16[2,256,512]{2,1,0:T(8,128)(2,1)S(1)}, u32[]{:S(2)}, u32[]{:S(2)}) collective-permute-start(bf16[2,256,512]{2,1,0:T(8,128)(2,1)} %get-tuple-element.50), channel_id=1, source_target_pairs={{0,4},{4,8},{8,12},{1,5},{5,9},{9,13},{2,6},{6,10},{10,14},{3,7},{... | collective-permute-start | bytes 1572872 | tf_op jit(solution)/shard_map/ppermute | solution.py:12
  23.0 16.8 %copy-start.9 = (bf16[2,256,512]{2,1,0:T(8,128)(2,1)S(1)}, bf16[2,256,512]{2,1,0:T(8,128)(2,1)}, u32[]{:S(2)}) copy-start(bf16[2,256,512]{2,1,0:T(8,128)(2,1)} %get-tuple-element.51) | copy-start | bytes 1572868
  37.2 44.1 %collective-permute-start.6 = (bf16[2,64,1536]{2,1,0:T(8,128)(2,1)S(1)}, bf16[2,64,1536]{2,1,0:T(8,128)(2,1)S(1)}, u32[]{:S(2)}, u32[]{:S(2)}) collective-permute-start(bf16[2,64,1536]{2,1,0:T(8,128)(2,1)S(1)} %slice.112), channel_id=1, source_target_pairs={{8,0},{9,1},{10,2},{11,3},{24,16},{25,17},{26,18},{27,19}} | collective-permute-start | bytes 1179656 | tf_op jit(solution)/shard_map/ppermute | solution.py:49
  38.5 42.9 %collective-permute-start.5 = (bf16[2,64,1536]{2,1,0:T(8,128)(2,1)S(1)}, bf16[2,64,1536]{2,1,0:T(8,128)(2,1)S(1)}, u32[]{:S(2)}, u32[]{:S(2)}) collective-permute-start(bf16[2,64,1536]{2,1,0:T(8,128)(2,1)S(1)} %slice.112), channel_id=1, source_target_pairs={{4,0},{5,1},{6,2},{7,3},{20,16},{21,17},{22,18},{23,19}} | collective-permute-start | bytes 1179656 | tf_op jit(solution)/shard_map/ppermute | solution.py:49
  39.8 41.5 %collective-permute-start.4 = (bf16[2,256,512]{2,1,0:T(8,128)(2,1)S(1)}, bf16[2,256,512]{2,1,0:T(8,128)(2,1)S(1)}, u32[]{:S(2)}, u32[]{:S(2)}) collective-permute-start(bf16[2,256,512]{2,1,0:T(8,128)(2,1)S(1)} %copy-done.9), channel_id=1, source_target_pairs={{0,4},{4,8},{8,12},{1,5},{5,9},{9,13},{2,6},{6,10},{10,14},{3,7},{... | collective-permute-start | bytes 1572872 | tf_op jit(solution)/shard_map/ppermute | solution.py:12
  44.4 102.6 %collective-permute-start.9 = (bf16[2,256,512]{2,1,0:T(8,128)(2,1)}, bf16[2,256,512]{2,1,0:T(8,128)(2,1)}, u32[]{:S(2)}, u32[]{:S(2)}) collective-permute-start(bf16[2,256,512]{2,1,0:T(8,128)(2,1)} %get-tuple-element.52), channel_id=1, source_target_pairs={{0,4},{4,8},{8,12},{1,5},{5,9},{9,13},{2,6},{6,10},{10,14},{3,7},{... | collective-permute-start | bytes 1572872 | tf_op jit(solution)/shard_map/ppermute | solution.py:12
  79.2 4.9 %copy-start.5 = (bf16[2,64,1536]{2,1,0:T(8,128)(2,1)}, bf16[2,64,1536]{2,1,0:T(8,128)(2,1)S(1)}, u32[]{:S(2)}) copy-start(bf16[2,64,1536]{2,1,0:T(8,128)(2,1)S(1)} %collective-permute-done.7) | copy-start | bytes 1179652
  79.2 36.9 %collective-permute-start.8 = (bf16[2,256,512]{2,1,0:T(8,128)(2,1)}, bf16[2,256,512]{2,1,0:T(8,128)(2,1)}, u32[]{:S(2)}, u32[]{:S(2)}) collective-permute-start(bf16[2,256,512]{2,1,0:T(8,128)(2,1)} %get-tuple-element.53), channel_id=1, source_target_pairs={{0,4},{4,8},{8,12},{1,5},{5,9},{9,13},{2,6},{6,10},{10,14},{3,7},{... | collective-permute-start | bytes 1572872 | tf_op jit(solution)/shard_map/ppermute | solution.py:12
  81.3 2.8 %copy-start.6 = (bf16[2,64,1536]{2,1,0:T(8,128)(2,1)}, bf16[2,64,1536]{2,1,0:T(8,128)(2,1)S(1)}, u32[]{:S(2)}) copy-start(bf16[2,64,1536]{2,1,0:T(8,128)(2,1)S(1)} %collective-permute-done.6) | copy-start | bytes 1179652
  81.3 2.8 %copy-start.7 = (bf16[2,64,1536]{2,1,0:T(8,128)(2,1)}, bf16[2,64,1536]{2,1,0:T(8,128)(2,1)S(1)}, u32[]{:S(2)}) copy-start(bf16[2,64,1536]{2,1,0:T(8,128)(2,1)S(1)} %collective-permute-done.5) | copy-start | bytes 1179652
  85.4 64.8 %reduce-scatter.7.cloned.1.call-start = ((), (), s32[]{:S(2)}) async-start(), calls=%async_computation.5 | async-start | bytes 1310720 | tf_op jit(solution)/shard_map/reduce_scatter | solution.py:79
  117.9 63.6 %reduce-scatter.9.cloned.1.call-start = ((), (), s32[]{:S(2)}) async-start(), calls=%async_computation.6 | async-start | bytes 1310720 | tf_op jit(solution)/shard_map/reduce_scatter | solution.py:79
  150.2 57.5 %reduce-scatter.11.cloned.1.call-start = ((), (), s32[]{:S(2)}) async-start(), calls=%async_computation.7 | async-start | bytes 1310720 | tf_op jit(solution)/shard_map/reduce_scatter | solution.py:79
  181.5 26.2 %copy-start.2 = (bf16[2,64,2048]{2,1,0:T(8,128)(2,1)S(1)}, bf16[2,64,2048]{2,1,0:T(8,128)(2,1)}, u32[]{:S(2)}) copy-start(bf16[2,64,2048]{2,1,0:T(8,128)(2,1)} %copy-done.1) | copy-start | bytes 1572868
  181.5 26.2 %copy-start.13 = (bf16[2,64,2048]{2,1,0:T(8,128)(2,1)S(1)}, bf16[2,64,2048]{2,1,0:T(8,128)(2,1)}, u32[]{:S(2)}) copy-start(bf16[2,64,2048]{2,1,0:T(8,128)(2,1)} %param.12) | copy-start | bytes 1572868
  181.5 26.2 %copy-start.14 = (f32[2,1,64,512]{3,2,0,1:T(8,128)S(1)}, f32[2,1,64,512]{3,2,0,1:T(8,128)}, u32[]{:S(2)}) copy-start(f32[2,1,64,512]{3,2,0,1:T(8,128)} %reduce-scatter.5.cloned.1.call-done) | copy-start | bytes 786436
  181.6 26.2 %copy-start.15 = (f32[2048]{0:T(1024)S(1)}, f32[2048]{0:T(1024)}, u32[]{:S(2)}) copy-start(f32[2048]{0:T(1024)} %param.13) | copy-start | bytes 24580
  (12 other events, 16.4 us)
Sparse Core Ops, SparseCore 0:
  85.5 26.0 reduce-scatter.4
  118.0 26.0 reduce-scatter.6
  150.4 26.0 reduce-scatter.8
  181.6 26.0 reduce-scatter.10

commit v4 on v3

--- a/solution.py
+++ b/solution.py
@@ -54,19 +54,24 @@
     )
     prev_keep = ((row_ids - tile_len)[None, :] < lengths[:, None])[:, :, None]
 
+    sent_rest = from_behind(history[:, :, chunk:], "seq", 1)
+    bounds_rest = [None] + [
+        slice(c * chunk - chunk, (c + 1) * chunk - chunk) for c in range(1, CHANNEL_CHUNKS)
+    ]
     head_parts = []
     own_parts = []
     for c in range(CHANNEL_CHUNKS):
         cols = slice(c * chunk, (c + 1) * chunk)
-        sent = from_behind(history[:, :, cols], "seq", 1)
-        if own_parts:
-            (sent, rest_each), _ = lax.optimization_barrier(((sent, rest_each), last_partial))
+        if c == 0:
+            sent = from_behind(history[:, :, cols], "seq", 1)
+            head_first = jnp.concatenate(first_each[::-1], axis=1)
+        else:
+            (sent_rest, rest_each), _ = lax.optimization_barrier(((sent_rest, rest_each), last_partial))
+            sent = sent_rest[:, :, bounds_rest[c]]
             rest_cols = slice((c - 1) * chunk, c * chunk)
             head_first = jnp.concatenate(
                 [part[:, :, rest_cols] for part in rest_each[::-1]], axis=1
             )
-        else:
-            head_first = jnp.concatenate(first_each[::-1], axis=1)
         head_c = jnp.where(position == 0, head_first, sent)
         head_parts.append(head_c)
         prev_live = jnp.where(prev_keep, head_c, jnp.zeros_like(head_c))

time: 218 us -> 224 us (1.028)
  local copies, waits for them, and re-layouts: 14.1 us -> 22.6 us
    slice x18 -> x12, local copies, waits for them, and re-layouts: 3.42 us -> 12 us  [per_device(): part[:, :, rest_cols]]
    ppermute x4 -> x2, starting transfers between devices: 14.6 us -> 13 us  [from_behind(): return lax.ppermute(block, axis, route)]
  transfers between devices with their start and end apart: 14 -> 12, of which waited for: 2 -> 2; matrix products, arithmetic and copies ran while one was open for 62% -> 64% of each run, Pallas kernels for 0% -> 0%
where the time goes in v4:
time: 224 us; the launch traced here: 223 us
  matrix products  119 us (53%)
  waiting for transfers between devices  36 us (16%)
  local copies, waits for them, and re-layouts  22.6 us (10%)
  starting transfers between devices  21.6 us (10%)
  between operations  14.2 us (6%)
  other arithmetic  9.63 us (4%)
    conv_general_dilated x4, matrix products, correlate(): lax.conv_general_dilated(signal, kernel[:, None, :], (1,), 'VALID', dimen...  116 us
    reduce_scatter x4, waiting for transfers between devices, per_device(): reduced = lax.psum_scatter(blocks, 'seq', scatter_dimension=1, tiled=True)  24.8 us
    ppermute x2, starting transfers between devices, from_behind(): return lax.ppermute(block, axis, route)  13 us
    slice x12, local copies, waits for them, and re-layouts, per_device(): part[:, :, rest_cols]  12 us
    ppermute x3, waiting for transfers between devices, per_device(): lax.ppermute(product_rev[:, :, :chunk], 'seq', [(d, 0)])  11.2 us
    select_n x4, other arithmetic, per_device(): prev_live = jnp.where(prev_keep, head_c, jnp.zeros_like(head_c))  5.95 us
  transfers between devices with their start and end apart: 12, of which 2 were waited for; matrix products, arithmetic and copies ran while one was open for 64% of the time, Pallas kernels for 0%

profile of v4, /device:TPU:0, one launch (start us, length us, event | category | flops | bytes accessed | tf_op | source)
XLA Modules:
  0.0 223.3 jit_solution(6969416812518614601)
XLA Ops:
  7.2 1.5 multiply_convert_fusion
  11.7 1.3 collective-permute-start.1
  13.0 1.3 collective-permute-start
  14.4 1.3 collective-permute-start.7
  15.7 6.5 %collective-permute-start.3 = (bf16[2,256,512]{2,1,0:T(8,128)(2,1)S(1)}, bf16[2,256,512]{2,1,0:T(8,128)(2,1)}, u32[]{:S(2)}, u32[]{:S(2)}) collective-permute-start(bf16[2,256,512]{2,1,0:T(8,128)(2,1)S(1)} %slice.88), channel_id=1, source_target_pairs={{0,4},{4,8},{8,12},{1,5},{5,9},{9,13},{2,6},{6,10},{10,14},{3,7},{... | collective-permute-start | bytes 1572872 | tf_op jit(solution)/shard_map/ppermute | solution.py:12
  26.0 11.2 %collective-permute-done.2 = bf16[2,64,512]{2,1,0:T(8,128)(2,1)} collective-permute-done((bf16[2,64,512]{2,1,0:T(8,128)(2,1)}, bf16[2,64,512]{2,1,0:T(8,128)(2,1)}, u32[]{:S(2)}, u32[]{:S(2)}) %collective-permute-start.2) | collective-permute-done | bytes 131104 | tf_op jit(solution)/shard_map/ppermute | solution.py:46
  38.4 1.3 collective-permute-start.5
  39.7 6.5 %collective-permute-start.4 = (bf16[2,256,1536]{2,1,0:T(8,128)(2,1)}, bf16[2,256,1536]{2,1,0:T(8,128)(2,1)}, u32[]{:S(2)}, u32[]{:S(2)}) collective-permute-start(bf16[2,256,1536]{2,1,0:T(8,128)(2,1)} %slice.91), channel_id=1, source_target_pairs={{0,4},{4,8},{8,12},{1,5},{5,9},{9,13},{2,6},{6,10},{10,14},{3,7},{... | collective-permute-start | bytes 4718600 | tf_op jit(solution)/shard_map/ppermute | solution.py:12
  46.2 2.1 broadcast_select_fusion.4
  48.4 29.1 %fusion.17 = f32[2,256,512]{2,0,1:T(2,128)S(1)} fusion(bf16[2,511,512]{2,1,0:T(8,128)(2,1)S(1)} %pad_maximum_fusion.1, bf16[256,1,512]{2,0,1:T(8,128)(2,1)S(1)} %get-tuple-element.52), kind=kOutput, calls=%fused_computation.26 | convolution fusion | flops 134217728 | bytes 2357248 | tf_op jit(solution)/shard_map/conv_general_dilated | solution.py:17
  81.1 1.3 broadcast_select_fusion.3
  82.5 29.1 %fusion.15 = f32[2,256,512]{2,0,1:T(2,128)S(1)} fusion(bf16[2,511,512]{2,1,0:T(8,128)(2,1)S(1)} %pad_maximum_fusion.2, bf16[256,1,512]{2,0,1:T(8,128)(2,1)S(1)} %copy-done.10), kind=kOutput, calls=%fused_computation.24 | convolution fusion | flops 134217728 | bytes 2357248 | tf_op jit(solution)/shard_map/conv_general_dilated | solution.py:17
  111.7 1.6 slice.100
  113.2 1.6 slice.101
  114.8 1.6 slice.102
  118.3 1.4 broadcast_select_fusion.2
  120.1 28.9 %fusion.13 = f32[2,256,512]{2,0,1:T(2,128)S(1)} fusion(bf16[2,511,512]{2,1,0:T(8,128)(2,1)S(1)} %pad_maximum_fusion.3, bf16[256,1,512]{2,0,1:T(8,128)(2,1)} %get-tuple-element.53), kind=kOutput, calls=%fused_computation.22 | convolution fusion | flops 134217728 | bytes 2357248 | tf_op jit(solution)/shard_map/conv_general_dilated | solution.py:17
  148.9 1.6 slice.107
  150.5 1.6 slice.108
  152.1 1.6 slice.109
  157.2 29.1 %fusion.11 = f32[2,256,512]{2,0,1:T(2,128)S(1)} fusion(bf16[2,511,512]{2,1,0:T(8,128)(2,1)S(1)} %pad_maximum_fusion.4, bf16[256,1,512]{2,0,1:T(8,128)(2,1)S(1)} %copy-done.9), kind=kOutput, calls=%fused_computation.20 | convolution fusion | flops 134217728 | bytes 2357248 | tf_op jit(solution)/shard_map/conv_general_dilated | solution.py:17
  187.7 1.6 pad_maximum_fusion
  189.3 24.7 %reduce-scatter.11.cloned.1.call-done = f32[2,1,64,512]{3,2,0,1:T(8,128)} async-done(((f32[2,4,64,512]{3,2,0,1:T(8,128)}), f32[2,1,64,512]{3,2,0,1:T(8,128)}) %reduce-scatter.11.cloned.1.call-update) | async-done | bytes 262160 | tf_op jit(solution)/shard_map/reduce_scatter | solution.py:84
  214.0 2.8 %fusion.2 = bf16[2,64,2048]{2,1,0:T(8,128)(2,1)} fusion(f32[2,64,512]{2,1,0:T(8,128)} %bitcast.38, f32[2,64,512]{2,1,0:T(8,128)} %bitcast.37, f32[2,64,512]{2,1,0:T(8,128)} %bitcast.36, f32[2,64,512]{2,1,0:T(8,128)S(1)} %bitcast.35, bf16[2,64,2048]{2,1,0:T(8,128)(2,1)S(1)} %copy-done.2, bf16[2,64,2048]{2,1,0:T(8,128)(2,1)S(1)} %copy-done.12, ...), kind=kOutput, calls=%fused_computation.3 | convolution fusion | flops 203694080 | bytes 2629632 | tf_op jit(solution)/shard_map/ik,rkc->ric/dot_general | solution.py:86
  (79 shorter events, 18.9 us)
Async XLA Ops:
  7.2 8.5 %copy-start = (bf16[2,256,2048]{2,1,0:T(8,128)(2,1)S(1)}, bf16[2,256,2048]{2,1,0:T(8,128)(2,1)}, u32[]{:S(2)}) copy-start(bf16[2,256,2048]{2,1,0:T(8,128)(2,1)} %param.7) | copy-start | bytes 6291460
  7.2 112.6 %reduce-scatter.5.cloned.1.call-start = ((), (), s32[]{:S(2)}) async-start(), calls=%async_computation.4 | async-start | bytes 1310720 | tf_op jit(solution)/shard_map/reduce_scatter | solution.py:84
  10.4 26.7 %collective-permute-start.2 = (bf16[2,64,512]{2,1,0:T(8,128)(2,1)}, bf16[2,64,512]{2,1,0:T(8,128)(2,1)}, u32[]{:S(2)}, u32[]{:S(2)}) collective-permute-start(bf16[2,64,512]{2,1,0:T(8,128)(2,1)} %slice.114), channel_id=1, source_target_pairs={{4,0},{5,1},{6,2},{7,3},{20,16},{21,17},{22,18},{23,19}} | collective-permute-start | bytes 393224 | tf_op jit(solution)/shard_map/ppermute | solution.py:46
  11.7 26.7 %collective-permute-start.1 = (bf16[2,64,512]{2,1,0:T(8,128)(2,1)}, bf16[2,64,512]{2,1,0:T(8,128)(2,1)}, u32[]{:S(2)}, u32[]{:S(2)}) collective-permute-start(bf16[2,64,512]{2,1,0:T(8,128)(2,1)} %slice.114), channel_id=1, source_target_pairs={{8,0},{9,1},{10,2},{11,3},{24,16},{25,17},{26,18},{27,19}} | collective-permute-start | bytes 393224 | tf_op jit(solution)/shard_map/ppermute | solution.py:46
  13.0 26.7 %collective-permute-start = (bf16[2,64,512]{2,1,0:T(8,128)(2,1)}, bf16[2,64,512]{2,1,0:T(8,128)(2,1)}, u32[]{:S(2)}, u32[]{:S(2)}) collective-permute-start(bf16[2,64,512]{2,1,0:T(8,128)(2,1)} %slice.114), channel_id=1, source_target_pairs={{12,0},{13,1},{14,2},{15,3},{28,16},{29,17},{30,18},{31,19}} | collective-permute-start | bytes 393224 | tf_op jit(solution)/shard_map/ppermute | solution.py:46
  14.4 9.2 %copy-start.11 = (s32[2]{0:T(128)S(1)}, s32[2]{0:T(128)}, u32[]{:S(2)}) copy-start(s32[2]{0:T(128)} %param.9) | copy-start | bytes 28
  14.4 64.7 %collective-permute-start.7 = (bf16[2,64,1536]{2,1,0:T(8,128)(2,1)S(1)}, bf16[2,64,1536]{2,1,0:T(8,128)(2,1)}, u32[]{:S(2)}, u32[]{:S(2)}) collective-permute-start(bf16[2,64,1536]{2,1,0:T(8,128)(2,1)S(1)} %slice.116), channel_id=1, source_target_pairs={{12,0},{13,1},{14,2},{15,3},{28,16},{29,17},{30,18},{31,19}} | collective-permute-start | bytes 1179656 | tf_op jit(solution)/shard_map/ppermute | solution.py:49
  15.7 30.5 %collective-permute-start.3 = (bf16[2,256,512]{2,1,0:T(8,128)(2,1)S(1)}, bf16[2,256,512]{2,1,0:T(8,128)(2,1)}, u32[]{:S(2)}, u32[]{:S(2)}) collective-permute-start(bf16[2,256,512]{2,1,0:T(8,128)(2,1)S(1)} %slice.88), channel_id=1, source_target_pairs={{0,4},{4,8},{8,12},{1,5},{5,9},{9,13},{2,6},{6,10},{10,14},{3,7},{... | collective-permute-start | bytes 1572872 | tf_op jit(solution)/shard_map/ppermute | solution.py:12
  23.8 1.2 copy-start.4
  37.1 41.9 %collective-permute-start.6 = (bf16[2,64,1536]{2,1,0:T(8,128)(2,1)S(1)}, bf16[2,64,1536]{2,1,0:T(8,128)(2,1)S(1)}, u32[]{:S(2)}, u32[]{:S(2)}) collective-permute-start(bf16[2,64,1536]{2,1,0:T(8,128)(2,1)S(1)} %slice.116), channel_id=1, source_target_pairs={{8,0},{9,1},{10,2},{11,3},{24,16},{25,17},{26,18},{27,19}} | collective-permute-start | bytes 1179656 | tf_op jit(solution)/shard_map/ppermute | solution.py:49
  38.4 40.7 %collective-permute-start.5 = (bf16[2,64,1536]{2,1,0:T(8,128)(2,1)S(1)}, bf16[2,64,1536]{2,1,0:T(8,128)(2,1)}, u32[]{:S(2)}, u32[]{:S(2)}) collective-permute-start(bf16[2,64,1536]{2,1,0:T(8,128)(2,1)S(1)} %slice.116), channel_id=1, source_target_pairs={{4,0},{5,1},{6,2},{7,3},{20,16},{21,17},{22,18},{23,19}} | collective-permute-start | bytes 1179656 | tf_op jit(solution)/shard_map/ppermute | solution.py:49
  39.7 39.4 %collective-permute-start.4 = (bf16[2,256,1536]{2,1,0:T(8,128)(2,1)}, bf16[2,256,1536]{2,1,0:T(8,128)(2,1)}, u32[]{:S(2)}, u32[]{:S(2)}) collective-permute-start(bf16[2,256,1536]{2,1,0:T(8,128)(2,1)} %slice.91), channel_id=1, source_target_pairs={{0,4},{4,8},{8,12},{1,5},{5,9},{9,13},{2,6},{6,10},{10,14},{3,7},{... | collective-permute-start | bytes 4718600 | tf_op jit(solution)/shard_map/ppermute | solution.py:12
  78.8 77.5 %reduce-scatter.7.cloned.1.call-start = ((), (), s32[]{:S(2)}) async-start(), calls=%async_computation.5 | async-start | bytes 1310720 | tf_op jit(solution)/shard_map/reduce_scatter | solution.py:84
  79.1 2.0 copy-start.8
  81.1 1.4 copy-start.10
  119.8 67.8 %reduce-scatter.9.cloned.1.call-start = ((), (), s32[]{:S(2)}) async-start(), calls=%async_computation.6 | async-start | bytes 1310720 | tf_op jit(solution)/shard_map/reduce_scatter | solution.py:84
  153.7 1.3 copy-start.5
  153.7 1.3 copy-start.6
  153.7 1.3 copy-start.7
  156.3 57.7 %reduce-scatter.11.cloned.1.call-start = ((), (), s32[]{:S(2)}) async-start(), calls=%async_computation.7 | async-start | bytes 1310720 | tf_op jit(solution)/shard_map/reduce_scatter | solution.py:84
  187.6 26.4 %copy-start.2 = (bf16[2,64,2048]{2,1,0:T(8,128)(2,1)S(1)}, bf16[2,64,2048]{2,1,0:T(8,128)(2,1)}, u32[]{:S(2)}) copy-start(bf16[2,64,2048]{2,1,0:T(8,128)(2,1)} %copy-done.1) | copy-start | bytes 1572868
  187.6 26.4 %copy-start.12 = (bf16[2,64,2048]{2,1,0:T(8,128)(2,1)S(1)}, bf16[2,64,2048]{2,1,0:T(8,128)(2,1)}, u32[]{:S(2)}) copy-start(bf16[2,64,2048]{2,1,0:T(8,128)(2,1)} %param.12) | copy-start | bytes 1572868
  187.6 26.4 %copy-start.13 = (f32[2,1,64,512]{3,2,0,1:T(8,128)S(1)}, f32[2,1,64,512]{3,2,0,1:T(8,128)}, u32[]{:S(2)}) copy-start(f32[2,1,64,512]{3,2,0,1:T(8,128)} %reduce-scatter.5.cloned.1.call-done) | copy-start | bytes 786436
  187.6 26.4 %copy-start.14 = (f32[2048]{0:T(1024)S(1)}, f32[2048]{0:T(1024)}, u32[]{:S(2)}) copy-start(f32[2048]{0:T(1024)} %param.13) | copy-start | bytes 24580
  (3 other events, 2.9 us)
Sparse Core Ops, SparseCore 0:
  78.9 26.2 reduce-scatter.4
  119.9 26.2 reduce-scatter.6
  156.5 26.2 reduce-scatter.8
  187.7 26.2 reduce-scatter.10

commit v5 on v1

--- a/solution.py
+++ b/solution.py
@@ -56,6 +56,7 @@
 
     head_parts = []
     own_parts = []
+    mixed_parts = []
     for c in range(CHANNEL_CHUNKS):
         cols = slice(c * chunk, (c + 1) * chunk)
         sent = from_behind(history[:, :, cols], "seq", 1)
@@ -78,10 +79,11 @@
             blocks, _ = lax.optimization_barrier((blocks, own_parts[-1]))
         reduced = lax.psum_scatter(blocks, "seq", scatter_dimension=1, tiled=True)
         own_parts.append(reduced[:, 0])
-    summed = jnp.concatenate(own_parts, axis=2)[:, ::-1]
-    product_float = product_own.astype(jnp.float32)
-    total = summed + skip_gain[None, None, :] * product_float
-    mixed = (outer_gate.astype(jnp.float32) * total).astype(jnp.bfloat16)
+        total = reduced[:, 0, ::-1] + skip_gain[None, None, cols] * product_own[
+            :, :, cols
+        ].astype(jnp.float32)
+        mixed_parts.append((outer_gate[:, :, cols].astype(jnp.float32) * total).astype(jnp.bfloat16))
+    mixed = jnp.concatenate(mixed_parts, axis=2)
     next_history = jnp.concatenate(head_parts, axis=2)
     return (mixed, next_history)
 

time: 217 us -> 267 us (1.23)
  waiting for transfers between devices: 37.2 us -> 72.5 us
  local copies, waits for them, and re-layouts: 14.6 us -> 29.8 us
  other arithmetic: 10.4 us -> 7.68 us
    reduce_scatter x4, waiting for transfers between devices: 24.6 us -> 72.4 us  [per_device(): reduced = lax.psum_scatter(blocks, 'seq', scatter_dimension=1, tiled=True)]
    ppermute x3, waiting for transfers between devices: 12.5 us -> 0.01 us  [per_device(): lax.ppermute(product_rev[:, :, :chunk], 'seq', [(d, 0)])]
    rev x1 -> x4, local copies, waits for them, and re-layouts: 0.45 us -> 7.01 us  [per_device(): reduced[:, 0, ::-1]]
    slice x18 -> x12, local copies, waits for them, and re-layouts: 3.41 us -> 8.26 us  [per_device(): part[:, :, rest_cols]]
    select_n x4, other arithmetic: 4.62 us -> 1.58 us  [per_device(): prev_live = jnp.where(prev_keep, head_c, jnp.zeros_like(head_c))]
  transfers between devices with their start and end apart: 14 -> 14, of which waited for: 2 -> 3; matrix products, arithmetic and copies ran while one was open for 62% -> 56% of each run, Pallas kernels for 0% -> 0%
where the time goes in v5:
time: 267 us; the launch traced here: 266 us
  matrix products  118 us (44%)
  waiting for transfers between devices  72.5 us (27%)
  local copies, waits for them, and re-layouts  29.8 us (11%)
  starting transfers between devices  23.9 us (9%)
  between operations  14.2 us (5%)
  other arithmetic  7.68 us (3%)
    conv_general_dilated x4, matrix products, correlate(): lax.conv_general_dilated(signal, kernel[:, None, :], (1,), 'VALID', dimen...  118 us
    reduce_scatter x4, waiting for transfers between devices, per_device(): reduced = lax.psum_scatter(blocks, 'seq', scatter_dimension=1, tiled=True)  72.4 us
    ppermute x4, starting transfers between devices, from_behind(): return lax.ppermute(block, axis, route)  16 us
    slice x12, local copies, waits for them, and re-layouts, per_device(): part[:, :, rest_cols]  8.26 us
    rev x4, local copies, waits for them, and re-layouts, per_device(): reduced[:, 0, ::-1]  7.01 us
  transfers between devices with their start and end apart: 14, of which 3 were waited for; matrix products, arithmetic and copies ran while one was open for 56% of the time, Pallas kernels for 0%

profile of v5, /device:TPU:0, one launch (start us, length us, event | category | flops | bytes accessed | tf_op | source)
XLA Modules:
  0.0 266.1 jit_solution(7914454773611521294)
XLA Ops:
  7.2 1.5 multiply_convert_fusion
  9.8 1.3 collective-permute-start.2
  11.1 1.3 collective-permute-start.1
  13.7 1.4 fusion.26
  15.1 3.7 %collective-permute-start.3 = (bf16[2,256,512]{2,1,0:T(8,128)(2,1)}, bf16[2,256,512]{2,1,0:T(8,128)(2,1)S(1)}, u32[]{:S(2)}, u32[]{:S(2)}) collective-permute-start(bf16[2,256,512]{2,1,0:T(8,128)(2,1)} %get-tuple-element.44), channel_id=1, source_target_pairs={{0,4},{4,8},{8,12},{1,5},{5,9},{9,13},{2,6},{6,10},{10,14},{3,7},{... | collective-permute-start | bytes 1572872 | tf_op jit(solution)/shard_map/ppermute | solution.py:12
  20.2 1.5 broadcast_select_fusion
  21.8 1.8 fusion.25
  27.2 6.3 %collective-permute-start.9 = (bf16[2,256,512]{2,1,0:T(8,128)(2,1)}, bf16[2,256,512]{2,1,0:T(8,128)(2,1)}, u32[]{:S(2)}, u32[]{:S(2)}) collective-permute-start(bf16[2,256,512]{2,1,0:T(8,128)(2,1)} %get-tuple-element.46), channel_id=1, source_target_pairs={{0,4},{4,8},{8,12},{1,5},{5,9},{9,13},{2,6},{6,10},{10,14},{3,7},{... | collective-permute-start | bytes 1572872 | tf_op jit(solution)/shard_map/ppermute | solution.py:12
  33.5 3.3 %collective-permute-start.4 = (bf16[2,256,512]{2,1,0:T(8,128)(2,1)}, bf16[2,256,512]{2,1,0:T(8,128)(2,1)}, u32[]{:S(2)}, u32[]{:S(2)}) collective-permute-start(bf16[2,256,512]{2,1,0:T(8,128)(2,1)} %get-tuple-element.45), channel_id=1, source_target_pairs={{0,4},{4,8},{8,12},{1,5},{5,9},{9,13},{2,6},{6,10},{10,14},{3,7},{... | collective-permute-start | bytes 1572872 | tf_op jit(solution)/shard_map/ppermute | solution.py:12
  37.8 29.1 %fusion.7 = f32[2,256,512]{2,0,1:T(2,128)S(1)} fusion(bf16[2,511,512]{2,1,0:T(8,128)(2,1)S(1)} %pad_maximum_fusion.1, bf16[256,1,512]{2,0,1:T(8,128)(2,1)S(1)} %get-tuple-element.54), kind=kOutput, calls=%fused_computation.15 | convolution fusion | flops 134217728 | bytes 2357248 | tf_op jit(solution)/shard_map/conv_general_dilated | solution.py:17
  68.4 2.7 %collective-permute-start.8 = (bf16[2,256,512]{2,1,0:T(8,128)(2,1)}, bf16[2,256,512]{2,1,0:T(8,128)(2,1)S(1)}, u32[]{:S(2)}, u32[]{:S(2)}) collective-permute-start(bf16[2,256,512]{2,1,0:T(8,128)(2,1)} %get-tuple-element.47), channel_id=1, source_target_pairs={{0,4},{4,8},{8,12},{1,5},{5,9},{9,13},{2,6},{6,10},{10,14},{3,7},{... | collective-permute-start | bytes 1572872 | tf_op jit(solution)/shard_map/ppermute | solution.py:12
  74.8 29.8 %fusion.5 = f32[2,256,512]{2,0,1:T(2,128)} fusion(bf16[2,511,512]{2,1,0:T(8,128)(2,1)S(1)} %pad_maximum_fusion.2, bf16[256,1,512]{2,0,1:T(8,128)(2,1)S(1)} %copy-done.8), kind=kOutput, calls=%fused_computation.13 | convolution fusion | flops 134217728 | bytes 2357248 | tf_op jit(solution)/shard_map/conv_general_dilated | solution.py:17
  108.3 29.8 %fusion.3 = f32[2,256,512]{2,0,1:T(2,128)} fusion(bf16[2,511,512]{2,1,0:T(8,128)(2,1)S(1)} %pad_maximum_fusion.3, bf16[256,1,512]{2,0,1:T(8,128)(2,1)S(1)} %copy-done.7), kind=kOutput, calls=%fused_computation.11 | convolution fusion | flops 134217728 | bytes 2357248 | tf_op jit(solution)/shard_map/conv_general_dilated | solution.py:17
  141.8 29.1 %fusion.1 = f32[2,256,512]{2,0,1:T(2,128)S(1)} fusion(bf16[2,511,512]{2,1,0:T(8,128)(2,1)S(1)} %pad_maximum_fusion.4, bf16[256,1,512]{2,0,1:T(8,128)(2,1)S(1)} %copy-done.6), kind=kOutput, calls=%fused_computation.9 | convolution fusion | flops 134217728 | bytes 2357248 | tf_op jit(solution)/shard_map/conv_general_dilated | solution.py:17
  172.3 1.4 copy.25
  174.9 1.4 copy.22
  177.5 1.6 pad_maximum_fusion
  179.1 1.8 rev.25
  180.9 19.6 %reduce-scatter.11.cloned.1.call-done = f32[2,1,64,512]{3,2,0,1:T(8,128)} async-done(((f32[2,4,64,512]{3,2,0,1:T(8,128)}), f32[2,1,64,512]{3,2,0,1:T(8,128)}) %reduce-scatter.11.cloned.1.call-update) | async-done | bytes 262160 | tf_op jit(solution)/shard_map/reduce_scatter | solution.py:80
  200.6 1.7 rev.31
  202.3 26.4 %reduce-scatter.9.cloned.1.call-done = f32[2,1,64,512]{3,2,0,1:T(8,128)} async-done(((f32[2,4,64,512]{3,2,0,1:T(8,128)}), f32[2,1,64,512]{3,2,0,1:T(8,128)}) %reduce-scatter.9.cloned.1.call-update) | async-done | bytes 262160 | tf_op jit(solution)/shard_map/reduce_scatter | solution.py:80
  228.7 1.7 rev.29
  230.4 26.3 %reduce-scatter.7.cloned.1.call-done = f32[2,1,64,512]{3,2,0,1:T(8,128)} async-done(((f32[2,4,64,512]{3,2,0,1:T(8,128)}), f32[2,1,64,512]{3,2,0,1:T(8,128)}) %reduce-scatter.7.cloned.1.call-update) | async-done | bytes 262160 | tf_op jit(solution)/shard_map/reduce_scatter | solution.py:80
  256.8 1.7 rev.27
  (80 shorter events, 25.6 us)
Async XLA Ops:
  7.2 6.6 %copy-start = (bf16[2,256,2048]{2,1,0:T(8,128)(2,1)S(1)}, bf16[2,256,2048]{2,1,0:T(8,128)(2,1)}, u32[]{:S(2)}) copy-start(bf16[2,256,2048]{2,1,0:T(8,128)(2,1)} %param.7) | copy-start | bytes 6291460
  7.2 171.9 %reduce-scatter.5.cloned.1.call-start = ((), (), s32[]{:S(2)}) async-start(), calls=%async_computation.4 | async-start | bytes 1310720 | tf_op jit(solution)/shard_map/reduce_scatter | solution.py:80
  9.8 10.3 %copy-start.10 = (s32[2]{0:T(128)S(1)}, s32[2]{0:T(128)}, u32[]{:S(2)}) copy-start(s32[2]{0:T(128)} %param.9) | copy-start | bytes 28
  9.8 14.7 %collective-permute-start.2 = (bf16[2,64,512]{2,1,0:T(8,128)(2,1)S(1)}, bf16[2,64,512]{2,1,0:T(8,128)(2,1)S(1)}, u32[]{:S(2)}, u32[]{:S(2)}) collective-permute-start(bf16[2,64,512]{2,1,0:T(8,128)(2,1)S(1)} %slice.158), channel_id=1, source_target_pairs={{4,0},{5,1},{6,2},{7,3},{20,16},{21,17},{22,18},{23,19}} | collective-permute-start | bytes 393224 | tf_op jit(solution)/shard_map/ppermute | solution.py:46
  11.1 14.7 %collective-permute-start.1 = (bf16[2,64,512]{2,1,0:T(8,128)(2,1)S(1)}, bf16[2,64,512]{2,1,0:T(8,128)(2,1)S(1)}, u32[]{:S(2)}, u32[]{:S(2)}) collective-permute-start(bf16[2,64,512]{2,1,0:T(8,128)(2,1)S(1)} %slice.158), channel_id=1, source_target_pairs={{8,0},{9,1},{10,2},{11,3},{24,16},{25,17},{26,18},{27,19}} | collective-permute-start | bytes 393224 | tf_op jit(solution)/shard_map/ppermute | solution.py:46
  12.4 14.7 %collective-permute-start = (bf16[2,64,512]{2,1,0:T(8,128)(2,1)S(1)}, bf16[2,64,512]{2,1,0:T(8,128)(2,1)S(1)}, u32[]{:S(2)}, u32[]{:S(2)}) collective-permute-start(bf16[2,64,512]{2,1,0:T(8,128)(2,1)S(1)} %slice.158), channel_id=1, source_target_pairs={{12,0},{13,1},{14,2},{15,3},{28,16},{29,17},{30,18},{31,19}} | collective-permute-start | bytes 393224 | tf_op jit(solution)/shard_map/ppermute | solution.py:46
  15.1 18.4 %collective-permute-start.3 = (bf16[2,256,512]{2,1,0:T(8,128)(2,1)}, bf16[2,256,512]{2,1,0:T(8,128)(2,1)S(1)}, u32[]{:S(2)}, u32[]{:S(2)}) collective-permute-start(bf16[2,256,512]{2,1,0:T(8,128)(2,1)} %get-tuple-element.44), channel_id=1, source_target_pairs={{0,4},{4,8},{8,12},{1,5},{5,9},{9,13},{2,6},{6,10},{10,14},{3,7},{... | collective-permute-start | bytes 1572872 | tf_op jit(solution)/shard_map/ppermute | solution.py:12
  18.8 49.5 %collective-permute-start.5 = (bf16[2,64,1536]{2,1,0:T(8,128)(2,1)S(1)}, bf16[2,64,1536]{2,1,0:T(8,128)(2,1)}, u32[]{:S(2)}, u32[]{:S(2)}) collective-permute-start(bf16[2,64,1536]{2,1,0:T(8,128)(2,1)S(1)} %slice.161), channel_id=1, source_target_pairs={{4,0},{5,1},{6,2},{7,3},{20,16},{21,17},{22,18},{23,19}} | collective-permute-start | bytes 1179656 | tf_op jit(solution)/shard_map/ppermute | solution.py:49
  21.8 1.9 copy-start.4
  24.5 46.5 %collective-permute-start.6 = (bf16[2,64,1536]{2,1,0:T(8,128)(2,1)S(1)}, bf16[2,64,1536]{2,1,0:T(8,128)(2,1)}, u32[]{:S(2)}, u32[]{:S(2)}) collective-permute-start(bf16[2,64,1536]{2,1,0:T(8,128)(2,1)S(1)} %slice.161), channel_id=1, source_target_pairs={{8,0},{9,1},{10,2},{11,3},{24,16},{25,17},{26,18},{27,19}} | collective-permute-start | bytes 1179656 | tf_op jit(solution)/shard_map/ppermute | solution.py:49
  25.8 45.2 %collective-permute-start.7 = (bf16[2,64,1536]{2,1,0:T(8,128)(2,1)S(1)}, bf16[2,64,1536]{2,1,0:T(8,128)(2,1)}, u32[]{:S(2)}, u32[]{:S(2)}) collective-permute-start(bf16[2,64,1536]{2,1,0:T(8,128)(2,1)S(1)} %slice.161), channel_id=1, source_target_pairs={{12,0},{13,1},{14,2},{15,3},{28,16},{29,17},{30,18},{31,19}} | collective-permute-start | bytes 1179656 | tf_op jit(solution)/shard_map/ppermute | solution.py:49
  27.2 110.9 %collective-permute-start.9 = (bf16[2,256,512]{2,1,0:T(8,128)(2,1)}, bf16[2,256,512]{2,1,0:T(8,128)(2,1)}, u32[]{:S(2)}, u32[]{:S(2)}) collective-permute-start(bf16[2,256,512]{2,1,0:T(8,128)(2,1)} %get-tuple-element.46), channel_id=1, source_target_pairs={{0,4},{4,8},{8,12},{1,5},{5,9},{9,13},{2,6},{6,10},{10,14},{3,7},{... | collective-permute-start | bytes 1572872 | tf_op jit(solution)/shard_map/ppermute | solution.py:12
  33.5 37.6 %collective-permute-start.4 = (bf16[2,256,512]{2,1,0:T(8,128)(2,1)}, bf16[2,256,512]{2,1,0:T(8,128)(2,1)}, u32[]{:S(2)}, u32[]{:S(2)}) collective-permute-start(bf16[2,256,512]{2,1,0:T(8,128)(2,1)} %get-tuple-element.45), channel_id=1, source_target_pairs={{0,4},{4,8},{8,12},{1,5},{5,9},{9,13},{2,6},{6,10},{10,14},{3,7},{... | collective-permute-start | bytes 1572872 | tf_op jit(solution)/shard_map/ppermute | solution.py:12
  68.3 132.3 %reduce-scatter.11.cloned.1.call-start = ((), (), s32[]{:S(2)}) async-start(), calls=%async_computation.7 | async-start | bytes 1310720 | tf_op jit(solution)/shard_map/reduce_scatter | solution.py:80
  68.4 36.2 %collective-permute-start.8 = (bf16[2,256,512]{2,1,0:T(8,128)(2,1)}, bf16[2,256,512]{2,1,0:T(8,128)(2,1)S(1)}, u32[]{:S(2)}, u32[]{:S(2)}) collective-permute-start(bf16[2,256,512]{2,1,0:T(8,128)(2,1)} %get-tuple-element.47), channel_id=1, source_target_pairs={{0,4},{4,8},{8,12},{1,5},{5,9},{9,13},{2,6},{6,10},{10,14},{3,7},{... | collective-permute-start | bytes 1572872 | tf_op jit(solution)/shard_map/ppermute | solution.py:12
  73.8 1.0 copy-start.8
  107.4 1.0 copy-start.7
  140.9 1.0 copy-start.6
  172.2 56.5 %reduce-scatter.9.cloned.1.call-start = ((), (), s32[]{:S(2)}) async-start(), calls=%async_computation.6 | async-start | bytes 1310720 | tf_op jit(solution)/shard_map/reduce_scatter | solution.py:80
  174.8 81.9 %reduce-scatter.7.cloned.1.call-start = ((), (), s32[]{:S(2)}) async-start(), calls=%async_computation.5 | async-start | bytes 1310720 | tf_op jit(solution)/shard_map/reduce_scatter | solution.py:80
  176.3 1.1 copy-start.9
  176.3 1.1 copy-start.3
  179.1 79.4 %copy-start.2 = (bf16[2,64,2048]{2,1,0:T(8,128)(2,1)S(1)}, bf16[2,64,2048]{2,1,0:T(8,128)(2,1)}, u32[]{:S(2)}) copy-start(bf16[2,64,2048]{2,1,0:T(8,128)(2,1)} %copy-done.1) | copy-start | bytes 1572868
  179.1 79.4 %copy-start.5 = (bf16[2,64,2048]{2,1,0:T(8,128)(2,1)S(1)}, bf16[2,64,2048]{2,1,0:T(8,128)(2,1)}, u32[]{:S(2)}) copy-start(bf16[2,64,2048]{2,1,0:T(8,128)(2,1)} %param.12) | copy-start | bytes 1572868
  (1 other events, 0.8 us)
Sparse Core Ops, SparseCore 0:
  68.4 31.3 reduce-scatter.4
  172.4 28.1 reduce-scatter.10
  202.9 25.7 reduce-scatter.8
  230.9 25.7 reduce-scatter.6

commit v6 on v1

--- a/solution.py
+++ b/solution.py
@@ -71,13 +71,15 @@
         head_parts.append(head_c)
         prev_live = jnp.where(prev_keep, head_c, jnp.zeros_like(head_c))
         segment = jnp.concatenate([prev_live, live_rows[:, : tile_len - 1, cols]], axis=1)
-        partial_rev = correlate(segment, filter_taps[:, cols])
+        signal = jnp.moveaxis(segment, 0, 1).reshape(1, 2 * tile_len - 1, requests * chunk)
+        taps = jnp.tile(filter_taps[:, cols], (1, requests))
+        partial_rev = correlate(signal, taps)
         last_partial = partial_rev
-        blocks = partial_rev.reshape(requests, n_seq, own_tokens, chunk)[:, ::-1]
+        blocks = partial_rev.reshape(n_seq, own_tokens, requests, chunk)[::-1]
         if own_parts:
             blocks, _ = lax.optimization_barrier((blocks, own_parts[-1]))
-        reduced = lax.psum_scatter(blocks, "seq", scatter_dimension=1, tiled=True)
-        own_parts.append(reduced[:, 0])
+        reduced = lax.psum_scatter(blocks, "seq", scatter_dimension=0, tiled=True)
+        own_parts.append(jnp.moveaxis(reduced[0], 1, 0))
     summed = jnp.concatenate(own_parts, axis=2)[:, ::-1]
     product_float = product_own.astype(jnp.float32)
     total = summed + skip_gain[None, None, :] * product_float

time: 217 us -> 256 us (1.18)
  local copies, waits for them, and re-layouts: 14.6 us -> 52.4 us
  waiting for transfers between devices: 37.2 us -> 26.1 us
  matrix products: 117 us -> 124 us
  starting transfers between devices: 23.9 us -> 27.7 us
    reshape x4 -> x12, local copies, waits for them, and re-layouts: 0.75 us -> 19.3 us  [the longest x4 15 us: per_device(): jnp.moveaxis(segment, 0, 1).reshape(1, 2 * tile_len - 1, requests * chunk)]
    ppermute x3, waiting for transfers between devices: 12.5 us -> 0.01 us  [per_device(): lax.ppermute(product_rev[:, :, :chunk], 'seq', [(d, 0)])]
    another operation x0 -> x8, local copies, waits for them, and re-layouts: none -> 8.53 us  [per_device(): taps = jnp.tile(filter_taps[:, cols], (1, requests))]
    conv_general_dilated x4, matrix products: 116 us -> 124 us  [correlate(): lax.conv_general_dilated(signal, kernel[:, None, :], (1,), 'VALID', dimen...]
    slice x18 -> x12, local copies, waits for them, and re-layouts: 3.41 us -> 8.32 us  [per_device(): part[:, :, rest_cols]]
    ppermute x4, starting transfers between devices: 15.4 us -> 19.4 us  [from_behind(): return lax.ppermute(block, axis, route)]
  transfers between devices with their start and end apart: 14 -> 14, of which waited for: 2 -> 1; matrix products, arithmetic and copies ran while one was open for 62% -> 71% of each run, Pallas kernels for 0% -> 0%
where the time goes in v6:
time: 256 us; the launch traced here: 255 us
  matrix products  124 us (48%)
  local copies, waits for them, and re-layouts  52.4 us (20%)
  starting transfers between devices  27.7 us (11%)
  waiting for transfers between devices  26.1 us (10%)
  between operations  14.3 us (6%)
  other arithmetic  10.6 us (4%)
    conv_general_dilated x4, matrix products, correlate(): lax.conv_general_dilated(signal, kernel[:, None, :], (1,), 'VALID', dimen...  124 us
    reduce_scatter x4, waiting for transfers between devices, per_device(): reduced = lax.psum_scatter(blocks, 'seq', scatter_dimension=0, tiled=True)  26 us
    ppermute x4, starting transfers between devices, from_behind(): return lax.ppermute(block, axis, route)  19.4 us
    reshape x4, local copies, waits for them, and re-layouts, per_device(): jnp.moveaxis(segment, 0, 1).reshape(1, 2 * tile_len - 1, requests * chunk)  15 us
    another operation x8, local copies, waits for them, and re-layouts, per_device(): taps = jnp.tile(filter_taps[:, cols], (1, requests))  8.53 us
    slice x12, local copies, waits for them, and re-layouts, per_device(): part[:, :, rest_cols]  8.32 us
  transfers between devices with their start and end apart: 14, of which 1 were waited for; matrix products, arithmetic and copies ran while one was open for 71% of the time, Pallas kernels for 0%

profile of v6, /device:TPU:0, one launch (start us, length us, event | category | flops | bytes accessed | tf_op | source)
XLA Modules:
  0.0 255.2 jit_solution(4118378886360475575)
XLA Ops:
  7.2 1.5 multiply_convert_fusion.1
  11.8 1.3 collective-permute-start.1
  15.7 1.4 fusion.6
  17.1 7.2 %collective-permute-start.3 = (bf16[2,256,512]{2,1,0:T(8,128)(2,1)}, bf16[2,256,512]{2,1,0:T(8,128)(2,1)}, u32[]{:S(2)}, u32[]{:S(2)}) collective-permute-start(bf16[2,256,512]{2,1,0:T(8,128)(2,1)} %get-tuple-element.50), channel_id=1, source_target_pairs={{0,4},{4,8},{8,12},{1,5},{5,9},{9,13},{2,6},{6,10},{10,14},{3,7},{... | collective-permute-start | bytes 1572872 | tf_op jit(solution)/shard_map/ppermute | solution.py:12
  24.4 1.5 broadcast_select_fusion
  25.9 2.6 %fusion.5 = (bf16[2,255,512]{2,1,0:T(8,128)(2,1)S(1)}, bf16[2,255,512]{2,1,0:T(8,128)(2,1)}, bf16[2,255,512]{2,1,0:T(8,128)(2,1)S(1)}, bf16[2,255,512]{2,1,0:T(8,128)(2,1)S(1)}) fusion(bf16[2,256,2048]{2,1,0:T(8,128)(2,1)} %broadcast_select_fusion), kind=kLoop, calls=%fused_computation.28 | loop fusion | bytes 4177920 | tf_op jit(solution)/shard_map/slice | solution.py:73
  30.6 2.1 copy.16
  32.9 2.1 copy.21
  35.2 2.1 copy.26
  37.4 2.1 copy.31
  42.1 3.1 %collective-permute-start.9 = (bf16[2,256,512]{2,1,0:T(8,128)(2,1)}, bf16[2,256,512]{2,1,0:T(8,128)(2,1)}, u32[]{:S(2)}, u32[]{:S(2)}) collective-permute-start(bf16[2,256,512]{2,1,0:T(8,128)(2,1)} %get-tuple-element.52), channel_id=1, source_target_pairs={{0,4},{4,8},{8,12},{1,5},{5,9},{9,13},{2,6},{6,10},{10,14},{3,7},{... | collective-permute-start | bytes 1572872 | tf_op jit(solution)/shard_map/ppermute | solution.py:12
  45.3 6.5 %collective-permute-start.4 = (bf16[2,256,512]{2,1,0:T(8,128)(2,1)}, bf16[2,256,512]{2,1,0:T(8,128)(2,1)}, u32[]{:S(2)}, u32[]{:S(2)}) collective-permute-start(bf16[2,256,512]{2,1,0:T(8,128)(2,1)} %get-tuple-element.51), channel_id=1, source_target_pairs={{0,4},{4,8},{8,12},{1,5},{5,9},{9,13},{2,6},{6,10},{10,14},{3,7},{... | collective-permute-start | bytes 1572872 | tf_op jit(solution)/shard_map/ppermute | solution.py:12
  51.8 2.1 broadcast_select_fusion.4
  54.5 3.7 %copy.15 = bf16[1,511,1024]{2,0,1:T(2,128)(2,1)} copy(bf16[1,511,1024]{1,2,0:T(8,128)(2,1)S(1)} %bitcast.42) | data formatting | bytes 2093056 | tf_op jit(solution)/shard_map/reshape | solution.py:74
  58.3 31.1 %fusion.10 = f32[256,1024]{1,0:T(8,128)} fusion(bf16[1,511,1024]{2,0,1:T(2,128)(2,1)} %copy.15, bf16[256,1,1024]{2,1,0:T(2,128)(2,1)S(1)} %copy-done.9), kind=kOutput, calls=%fused_computation.33 | convolution fusion | flops 134217728 | bytes 2619392 | tf_op jit(solution)/shard_map/conv_general_dilated | solution.py:17
  89.4 2.5 collective-permute-start.8
  96.3 3.7 %copy.20 = bf16[1,511,1024]{2,0,1:T(2,128)(2,1)} copy(bf16[1,511,1024]{1,2,0:T(8,128)(2,1)S(1)} %bitcast.43) | data formatting | bytes 2093056 | tf_op jit(solution)/shard_map/reshape | solution.py:74
  102.8 31.1 %fusion.9 = f32[256,1024]{1,0:T(8,128)} fusion(bf16[1,511,1024]{2,0,1:T(2,128)(2,1)} %copy.20, bf16[256,1,1024]{2,1,0:T(2,128)(2,1)S(1)} %copy-done.8), kind=kOutput, calls=%fused_computation.32 | convolution fusion | flops 134217728 | bytes 2619392 | tf_op jit(solution)/shard_map/conv_general_dilated | solution.py:17
  137.5 3.7 %copy.25 = bf16[1,511,1024]{2,0,1:T(2,128)(2,1)} copy(bf16[1,511,1024]{1,2,0:T(8,128)(2,1)S(1)} %bitcast.44) | data formatting | bytes 2093056 | tf_op jit(solution)/shard_map/reshape | solution.py:74
  144.0 31.1 %fusion.8 = f32[256,1024]{1,0:T(8,128)} fusion(bf16[1,511,1024]{2,0,1:T(2,128)(2,1)} %copy.25, bf16[256,1,1024]{2,1,0:T(2,128)(2,1)S(1)} %copy-done.7), kind=kOutput, calls=%fused_computation.31 | convolution fusion | flops 134217728 | bytes 2619392 | tf_op jit(solution)/shard_map/conv_general_dilated | solution.py:17
  178.8 3.7 %copy.30 = bf16[1,511,1024]{2,0,1:T(2,128)(2,1)} copy(bf16[1,511,1024]{1,2,0:T(8,128)(2,1)S(1)} %bitcast.45) | data formatting | bytes 2093056 | tf_op jit(solution)/shard_map/reshape | solution.py:74
  185.2 30.5 %convolution_reduce_fusion = f32[256,1024]{1,0:T(8,128)S(1)} fusion(bf16[1,511,1024]{2,0,1:T(2,128)(2,1)} %copy.30, bf16[256,1,1024]{2,1,0:T(2,128)(2,1)S(1)} %copy-done.6), kind=kOutput, calls=%fused_computation.11 | convolution fusion | flops 134217728 | bytes 2619392 | tf_op jit(solution)/shard_map/conv_general_dilated | solution.py:17
  218.4 1.6 pad_maximum_fusion
  220.0 26.0 %reduce-scatter.11.cloned.1.call-done = f32[1,64,2,512]{3,1,2,0:T(8,128)} async-done(((f32[4,64,2,512]{3,1,2,0:T(8,128)}), f32[1,64,2,512]{3,1,2,0:T(8,128)}) %reduce-scatter.11.cloned.1.call-update) | async-done | bytes 262160 | tf_op jit(solution)/shard_map/reduce_scatter | solution.py:81
  (120 shorter events, 36.3 us)
Async XLA Ops:
  7.2 8.5 %copy-start = (bf16[2,256,2048]{2,1,0:T(8,128)(2,1)S(1)}, bf16[2,256,2048]{2,1,0:T(8,128)(2,1)}, u32[]{:S(2)}) copy-start(bf16[2,256,2048]{2,1,0:T(8,128)(2,1)} %param.7) | copy-start | bytes 6291460
  7.2 136.3 %reduce-scatter.5.cloned.1.call-start = ((), (), s32[]{:S(2)}) async-start(), calls=%async_computation.4 | async-start | bytes 1310720 | tf_op jit(solution)/shard_map/reduce_scatter | solution.py:81
  10.5 29.1 %collective-permute-start.2 = (bf16[2,64,512]{2,1,0:T(8,128)(2,1)}, bf16[2,64,512]{2,1,0:T(8,128)(2,1)}, u32[]{:S(2)}, u32[]{:S(2)}) collective-permute-start(bf16[2,64,512]{2,1,0:T(8,128)(2,1)} %slice.110), channel_id=1, source_target_pairs={{4,0},{5,1},{6,2},{7,3},{20,16},{21,17},{22,18},{23,19}} | collective-permute-start | bytes 393224 | tf_op jit(solution)/shard_map/ppermute | solution.py:46
  11.8 29.1 %collective-permute-start.1 = (bf16[2,64,512]{2,1,0:T(8,128)(2,1)}, bf16[2,64,512]{2,1,0:T(8,128)(2,1)}, u32[]{:S(2)}, u32[]{:S(2)}) collective-permute-start(bf16[2,64,512]{2,1,0:T(8,128)(2,1)} %slice.110), channel_id=1, source_target_pairs={{8,0},{9,1},{10,2},{11,3},{24,16},{25,17},{26,18},{27,19}} | collective-permute-start | bytes 393224 | tf_op jit(solution)/shard_map/ppermute | solution.py:46
  13.1 29.1 %collective-permute-start = (bf16[2,64,512]{2,1,0:T(8,128)(2,1)}, bf16[2,64,512]{2,1,0:T(8,128)(2,1)}, u32[]{:S(2)}, u32[]{:S(2)}) collective-permute-start(bf16[2,64,512]{2,1,0:T(8,128)(2,1)} %slice.110), channel_id=1, source_target_pairs={{12,0},{13,1},{14,2},{15,3},{28,16},{29,17},{30,18},{31,19}} | collective-permute-start | bytes 393224 | tf_op jit(solution)/shard_map/ppermute | solution.py:46
  14.4 9.9 %copy-start.20 = (s32[2]{0:T(128)S(1)}, s32[2]{0:T(128)}, u32[]{:S(2)}) copy-start(s32[2]{0:T(128)} %param.9) | copy-start | bytes 28
  14.4 75.0 %collective-permute-start.5 = (bf16[2,64,1536]{2,1,0:T(8,128)(2,1)S(1)}, bf16[2,64,1536]{2,1,0:T(8,128)(2,1)}, u32[]{:S(2)}, u32[]{:S(2)}) collective-permute-start(bf16[2,64,1536]{2,1,0:T(8,128)(2,1)S(1)} %slice.112), channel_id=1, source_target_pairs={{4,0},{5,1},{6,2},{7,3},{20,16},{21,17},{22,18},{23,19}} | collective-permute-start | bytes 1179656 | tf_op jit(solution)/shard_map/ppermute | solution.py:49
  17.1 28.2 %collective-permute-start.3 = (bf16[2,256,512]{2,1,0:T(8,128)(2,1)}, bf16[2,256,512]{2,1,0:T(8,128)(2,1)}, u32[]{:S(2)}, u32[]{:S(2)}) collective-permute-start(bf16[2,256,512]{2,1,0:T(8,128)(2,1)} %get-tuple-element.50), channel_id=1, source_target_pairs={{0,4},{4,8},{8,12},{1,5},{5,9},{9,13},{2,6},{6,10},{10,14},{3,7},{... | collective-permute-start | bytes 1572872 | tf_op jit(solution)/shard_map/ppermute | solution.py:12
  29.4 3.3 %copy-start.14 = (bf16[256,512]{1,0:T(8,128)(2,1)S(1)}, bf16[256,512]{1,0:T(8,128)(2,1)}, u32[]{:S(2)}) copy-start(bf16[256,512]{1,0:T(8,128)(2,1)} %get-tuple-element.55) | copy-start | bytes 786436
  39.5 52.4 %collective-permute-start.6 = (bf16[2,64,1536]{2,1,0:T(8,128)(2,1)S(1)}, bf16[2,64,1536]{2,1,0:T(8,128)(2,1)}, u32[]{:S(2)}, u32[]{:S(2)}) collective-permute-start(bf16[2,64,1536]{2,1,0:T(8,128)(2,1)S(1)} %slice.112), channel_id=1, source_target_pairs={{8,0},{9,1},{10,2},{11,3},{24,16},{25,17},{26,18},{27,19}} | collective-permute-start | bytes 1179656 | tf_op jit(solution)/shard_map/ppermute | solution.py:49
  40.8 51.1 %collective-permute-start.7 = (bf16[2,64,1536]{2,1,0:T(8,128)(2,1)S(1)}, bf16[2,64,1536]{2,1,0:T(8,128)(2,1)}, u32[]{:S(2)}, u32[]{:S(2)}) collective-permute-start(bf16[2,64,1536]{2,1,0:T(8,128)(2,1)S(1)} %slice.112), channel_id=1, source_target_pairs={{12,0},{13,1},{14,2},{15,3},{28,16},{29,17},{30,18},{31,19}} | collective-permute-start | bytes 1179656 | tf_op jit(solution)/shard_map/ppermute | solution.py:49
  42.1 133.0 %collective-permute-start.9 = (bf16[2,256,512]{2,1,0:T(8,128)(2,1)}, bf16[2,256,512]{2,1,0:T(8,128)(2,1)}, u32[]{:S(2)}, u32[]{:S(2)}) collective-permute-start(bf16[2,256,512]{2,1,0:T(8,128)(2,1)} %get-tuple-element.52), channel_id=1, source_target_pairs={{0,4},{4,8},{8,12},{1,5},{5,9},{9,13},{2,6},{6,10},{10,14},{3,7},{... | collective-permute-start | bytes 1572872 | tf_op jit(solution)/shard_map/ppermute | solution.py:12
  45.3 46.7 %collective-permute-start.4 = (bf16[2,256,512]{2,1,0:T(8,128)(2,1)}, bf16[2,256,512]{2,1,0:T(8,128)(2,1)}, u32[]{:S(2)}, u32[]{:S(2)}) collective-permute-start(bf16[2,256,512]{2,1,0:T(8,128)(2,1)} %get-tuple-element.51), channel_id=1, source_target_pairs={{0,4},{4,8},{8,12},{1,5},{5,9},{9,13},{2,6},{6,10},{10,14},{3,7},{... | collective-permute-start | bytes 1572872 | tf_op jit(solution)/shard_map/ppermute | solution.py:12
  54.5 3.8 %copy-start.9 = (bf16[256,1,1024]{2,1,0:T(2,128)(2,1)S(1)}, bf16[256,1,1024]{2,1,0:T(2,128)(2,1)}, u32[]{:S(2)}) copy-start(bf16[256,1,1024]{2,1,0:T(2,128)(2,1)} %copy.16) | copy-start | bytes 1572868
  89.4 44.5 %collective-permute-start.8 = (bf16[2,256,512]{2,1,0:T(8,128)(2,1)}, bf16[2,256,512]{2,1,0:T(8,128)(2,1)S(1)}, u32[]{:S(2)}, u32[]{:S(2)}) collective-permute-start(bf16[2,256,512]{2,1,0:T(8,128)(2,1)} %get-tuple-element.53), channel_id=1, source_target_pairs={{0,4},{4,8},{8,12},{1,5},{5,9},{9,13},{2,6},{6,10},{10,14},{3,7},{... | collective-permute-start | bytes 1572872 | tf_op jit(solution)/shard_map/ppermute | solution.py:12
  96.3 3.8 %copy-start.11 = (f32[256,1024]{1,0:T(8,128)S(1)}, f32[256,1024]{1,0:T(8,128)}, u32[]{:S(2)}) copy-start(f32[256,1024]{1,0:T(8,128)} %fusion.10) | copy-start | bytes 3145732
  102.3 82.4 %reduce-scatter.7.cloned.1.call-start = ((), (), s32[]{:S(2)}) async-start(), calls=%async_computation.5 | async-start | bytes 1310720 | tf_op jit(solution)/shard_map/reduce_scatter | solution.py:81
  137.5 3.8 %copy-start.13 = (f32[256,1024]{1,0:T(8,128)S(1)}, f32[256,1024]{1,0:T(8,128)}, u32[]{:S(2)}) copy-start(f32[256,1024]{1,0:T(8,128)} %fusion.9) | copy-start | bytes 3145732
  143.5 74.4 %reduce-scatter.9.cloned.1.call-start = ((), (), s32[]{:S(2)}) async-start(), calls=%async_computation.6 | async-start | bytes 1310720 | tf_op jit(solution)/shard_map/reduce_scatter | solution.py:81
  178.8 3.8 %copy-start.12 = (f32[256,1024]{1,0:T(8,128)S(1)}, f32[256,1024]{1,0:T(8,128)}, u32[]{:S(2)}) copy-start(f32[256,1024]{1,0:T(8,128)} %fusion.8) | copy-start | bytes 3145732
  184.7 61.3 %reduce-scatter.11.cloned.1.call-start = ((), (), s32[]{:S(2)}) async-start(), calls=%async_computation.7 | async-start | bytes 1310720 | tf_op jit(solution)/shard_map/reduce_scatter | solution.py:81
  218.4 27.7 %copy-start.16 = (f32[1,64,2,512]{3,1,2,0:T(8,128)S(1)}, f32[1,64,2,512]{3,1,2,0:T(8,128)}, u32[]{:S(2)}) copy-start(f32[1,64,2,512]{3,1,2,0:T(8,128)} %reduce-scatter.5.cloned.1.call-done) | copy-start | bytes 786436
  218.4 27.7 %copy-start.17 = (f32[1,64,2,512]{3,1,2,0:T(8,128)S(1)}, f32[1,64,2,512]{3,1,2,0:T(8,128)}, u32[]{:S(2)}) copy-start(f32[1,64,2,512]{3,1,2,0:T(8,128)} %reduce-scatter.7.cloned.1.call-done) | copy-start | bytes 786436
  218.4 27.7 %copy-start.18 = (f32[1,64,2,512]{3,1,2,0:T(8,128)S(1)}, f32[1,64,2,512]{3,1,2,0:T(8,128)}, u32[]{:S(2)}) copy-start(f32[1,64,2,512]{3,1,2,0:T(8,128)} %reduce-scatter.9.cloned.1.call-done) | copy-start | bytes 786436
  (11 other events, 18.9 us)
Sparse Core Ops, SparseCore 0:
  102.4 26.8 reduce-scatter.4
  143.6 26.8 reduce-scatter.6
  184.8 27.9 reduce-scatter.8
  218.1 27.9 reduce-scatter.10
